TPU v7x, 32 devices: a whole 2x2x4 slice. The times are simulated.
32 devices in a mesh: search: 4 (over y, core), net: 8 (over z, x).
Axes of the slice: x: 2, y: 2, z: 4, core: 2. Of those that a mesh axis runs over, the one named last changes fastest.
Arguments:
- states: bfloat16 [4096, 11552], P(('search', 'net')), may hold values from -6 to 6
- counts: int32 [32], P(('search', 'net')), may hold values from 1 to 128, 1024 in all
- owners: int32 [4096], P(('search', 'net')), may hold values from 0 to 255
- legal: int32 [4096, 8, 361], P(('search', 'net')), may hold values 0 or 1
- in_weight: bfloat16 [3, 3, 32, 256], replicated, may hold values from -0.375 to 0.375
- mid_weight: bfloat16 [1, 3, 3, 256, 256], replicated, may hold values from -0.125 to 0.125
- out_weight: bfloat16 [1, 3, 3, 256, 256], replicated, may hold values from -0.125 to 0.125
- policy_weight: bfloat16 [256, 8], replicated, may hold values from -0.75 to 0.75
- pass_weight: bfloat16 [256, 8], replicated, may hold values from -1.5 to 1.5
- value_weight: bfloat16 [256], replicated, may hold values from -1.5 to 1.5
- logit_scale: float32 [8], replicated, may hold values from 0.25 to 4
Outputs:
- priors: float32 [4096, 8, 362], P(('search', 'net'))
- leaf_values: float32 [4096], P(('search', 'net'))
- tree_value: float32 [256], P(('search', 'net'))
Inputs may be any that keep to these rules, and one draw needn't show every extreme that they name: counts sum to exactly 32 times the number of devices, and one device holds 128 live leaves.
All inputs are finite; a program needn't handle non-finite values. No bound on the sum of `legal` on one device may be relied on, other than what follows from the above.
Results may differ from a plain program's by a relative error of at most 0.03.
Values may be sent and summed in bfloat16 or wider, within the bound.
No kernel may reach another device: no remote copies, remote signals or barrier semaphores. Data moves between devices by JAX's collectives and lax.ppermute only.
A program may use at most 128 MiB of HBM per device.

v0:
```python
import jax
import jax.numpy as jnp
from jax import lax
from jax.sharding import PartitionSpec as P

SIDE = 19
BOARD = 361
PLANES = 32
FACT = 8
TREE_DEV = 8


def convolve(inputs, kernel):
    return lax.conv_general_dilated(
        inputs,
        kernel,
        (1, 1),
        "SAME",
        dimension_numbers=("NHWC", "HWIO", "NHWC"),
        preferred_element_type=jnp.float32,
    )


def evaluate(batch, in_weight, mid_weight, out_weight, policy_weight, pass_weight, value_weight):
    leaves = batch.shape[0]
    board = batch.reshape(leaves, SIDE, SIDE, PLANES)
    hidden = jax.nn.relu(convolve(board, in_weight)).astype(jnp.bfloat16)
    inner = jax.nn.relu(convolve(hidden, mid_weight[0])).astype(jnp.bfloat16)
    hidden = jax.nn.relu(hidden.astype(jnp.float32) + convolve(inner, out_weight[0])).astype(
        jnp.bfloat16
    )
    cells = jnp.einsum(
        "bhwc,cf->bfhw", hidden, policy_weight, preferred_element_type=jnp.float32
    ).reshape(leaves, FACT, BOARD)
    pooled = jnp.mean(hidden, axis=(1, 2), dtype=jnp.float32)
    passing = jnp.dot(pooled, pass_weight.astype(jnp.float32), precision=lax.Precision.HIGHEST)
    logits = jnp.concatenate([cells, passing[:, :, None]], axis=2).astype(jnp.bfloat16)
    values = jnp.tanh(
        jnp.dot(pooled, value_weight.astype(jnp.float32), precision=lax.Precision.HIGHEST)
    ).astype(jnp.bfloat16)
    return (logits, values)


def masked_priors(logits, legal, logit_scale):
    scaled = logit_scale[None, :, None] * logits.astype(jnp.float32)
    allowed = jnp.concatenate(
        [legal > 0, jnp.ones(legal.shape[:2] + (1,), dtype=jnp.bool_)], axis=2
    )
    peak = jnp.max(jnp.where(allowed, scaled, -1e30), axis=2, keepdims=True)
    weights = jnp.exp(jnp.where(allowed, scaled - peak, -1e30))
    return weights / jnp.sum(weights, axis=2, keepdims=True)


def body(
    states,
    counts,
    owners,
    legal,
    in_weight,
    mid_weight,
    out_weight,
    policy_weight,
    pass_weight,
    value_weight,
    logit_scale,
):
    slot_count = states.shape[0]
    own_count = counts[0]
    slot_index = jnp.arange(slot_count, dtype=jnp.int32)
    returned_logits, returned_values = evaluate(
        states, in_weight, mid_weight, out_weight, policy_weight, pass_weight, value_weight
    )
    alive = slot_index < own_count
    priors = masked_priors(returned_logits, legal, logit_scale) * alive[:, None, None].astype(
        jnp.float32
    )
    leaf_values = jnp.where(alive, returned_values.astype(jnp.float32), 0.0)
    tree_total = TREE_DEV * lax.axis_size(("search", "net"))
    onehot = (owners[:, None] == jnp.arange(tree_total, dtype=jnp.int32)[None, :]).astype(
        jnp.float32
    )
    partial_sums = jnp.dot(leaf_values, onehot, precision=lax.Precision.HIGHEST)
    tree_value = lax.psum_scatter(partial_sums, ("search", "net"), scatter_dimension=0, tiled=True)
    return (priors, leaf_values, tree_value)


def solution(mesh):
    in_specs = (
        P(("search", "net"), None),
        P(("search", "net")),
        P(("search", "net")),
        P(("search", "net"), None, None),
        P(),
        P(),
        P(),
        P(),
        P(),
        P(),
        P(),
    )
    out_specs = (P(("search", "net"), None, None), P(("search", "net")), P(("search", "net")))
    return jax.shard_map(body, mesh=mesh, in_specs=in_specs, out_specs=out_specs, check_vma=False)
```

profile of v0, /device:TPU:0, one launch (start us, length us, event | category | flops | bytes accessed | tf_op | source)
XLA Modules:
  0.0 207.4 jit_solution(9432132262252542123)
XLA Ops:
  0.6 0.0 copy-start
  0.6 1.8 copy-done
  2.5 17.2 %maximum_convert_fusion.2 = bf16[128,19,19,256]{3,0,2,1:T(8,128)(2,1)} fusion(bf16[128,19,19,32]{0,3,2,1:T(8,128)(2,1)S(1)} %bitcast.44, bf16[3,3,32,256]{3,2,1,0:T(8,128)(2,1)} %param.15), kind=kOutput, calls=%fused_computation.3 | convolution fusion | flops 6367543296 | bytes 26763264 | tf_op jit(solution)/shard_map/conv_general_dilated | solution.py:14
  19.6 59.2 %fusion.4 = bf16[128,19,19,256]{3,0,2,1:T(8,128)(2,1)S(1)} fusion(bf16[128,19,19,256]{3,0,2,1:T(8,128)(2,1)} %maximum_convert_fusion.2, bf16[1,3,3,256,256]{4,3,2,1,0:T(8,128)(2,1)} %param.16), kind=kOutput, calls=%fused_computation.13 | convolution fusion | flops 50751078400 | bytes 48496640 | tf_op jit(solution)/shard_map/conv_general_dilated | solution.py:14
  78.9 0.0 copy-start.9
  78.9 12.1 %maximum_convert_fusion.5.clone.4 = bf16[128,19,19,256]{3,0,2,1:T(8,128)(2,1)} fusion(bf16[128,19,19,256]{3,0,2,1:T(8,128)(2,1)S(1)} %fusion.4), kind=kLoop, calls=%fused_computation.2.clone.clone.clone.clone.clone.clone.1 | loop fusion | flops 35487744 | bytes 47316992 | tf_op jit(solution)/shard_map/reduce_sum | solution.py:35
  91.0 0.0 copy-done.9
  91.0 0.0 copy-start.7
  91.0 0.0 copy-start.6
  91.0 62.1 %convert_reduce_fusion = (f32[128,256]{1,0:T(8,128)S(1)}, bf16[128,19,19,256]{3,0,2,1:T(8,128)(2,1)S(1)}) fusion(bf16[1,3,3,256,256]{4,3,2,1,0:T(8,128)(2,1)S(1)} %copy-done.9, bf16[128,19,19,256]{3,0,2,1:T(8,128)(2,1)} %maximum_convert_fusion.2, bf16[128,19,19,256]{3,0,2,1:T(8,128)(2,1)} %maximum_convert_fusion.5.clone.4), kind=kOutput, calls=%fused_computation | convolution fusion | flops 50822021120 | bytes 72286208 | tf_op jit(solution)/shard_map/conv_general_dilated | solution.py:14
  153.2 0.0 copy-start.3
  153.2 0.0 copy-done.7
  153.2 0.2 fusion.6
  153.3 0.5 copy-done.3
  153.8 0.0 copy-done.6
  153.8 0.0 copy-start.2
  153.8 6.2 %convolution_convert_fusion = bf16[128,19,19,8]{0,3,2,1:T(8,128)(2,1)S(1)} fusion(bf16[128,19,19,256]{3,0,2,1:T(8,128)(2,1)S(1)} %get-tuple-element.4, bf16[256,8]{0,1:T(8,128)(2,1)S(1)} %copy-done.6), kind=kOutput, calls=%fused_computation.10 | convolution fusion | flops 189637632 | bytes 24401920 | tf_op jit(solution)/shard_map/bhwc,cf->bfhw/dot_general | solution.py:32
  160.0 0.0 copy-start.5
  160.0 0.0 copy-done.2
  160.0 0.2 broadcast_compare_fusion
  160.2 0.5 copy-done.5
  160.7 0.6 select_reduce_fusion
  161.3 0.0 copy-start.1
  161.3 0.5 fusion.2
  161.8 0.0 copy-start.10
  161.8 0.0 copy-start.4
  161.8 0.0 copy-start.11
  162.7 1.7 divide_multiply_fusion
  164.4 0.0 copy-done.10
  164.4 0.0 copy-done.4
  164.4 0.2 fusion.10
  164.6 0.0 copy-done.11
  164.6 0.0 copy-start.8
  164.6 0.2 fusion.11
  164.8 42.0 %all-reduce.1 = f32[256]{0:T(256)S(1)} all-reduce(f32[256]{0:T(256)S(1)} %bitcast.48), channel_id=2, replica_groups=mesh['search'=4,'net'=8] {'search','net'}, use_global_device_ids=true, to_apply=%region_3.4.clone | all-reduce | flops 256 | bytes 2048
  206.8 0.6 dynamic-slice
  207.4 0.0 copy-done.8
  207.4 0.0 copy-done.1
  (2 shorter events, 0.0 us)
Async XLA Ops:
  0.6 1.8 copy-start
  78.9 12.2 %copy-start.9 = (bf16[1,3,3,256,256]{4,3,2,1,0:T(8,128)(2,1)S(1)}, bf16[1,3,3,256,256]{4,3,2,1,0:T(8,128)(2,1)}, u32[]{:S(2)}) copy-start(bf16[1,3,3,256,256]{4,3,2,1,0:T(8,128)(2,1)} %param.17) | copy-start | bytes 3538948
  91.0 62.1 %copy-start.7 = (bf16[256,8]{0,1:T(8,128)(2,1)S(1)}, bf16[256,8]{0,1:T(8,128)(2,1)}, u32[]{:S(2)}) copy-start(bf16[256,8]{0,1:T(8,128)(2,1)} %param.19) | copy-start | bytes 12292
  91.0 62.8 %copy-start.6 = (bf16[256,8]{0,1:T(8,128)(2,1)S(1)}, bf16[256,8]{0,1:T(8,128)(2,1)}, u32[]{:S(2)}) copy-start(bf16[256,8]{0,1:T(8,128)(2,1)} %param.18) | copy-start | bytes 12292
  153.2 0.6 copy-start.3
  153.8 6.2 %copy-start.2 = (s32[128,8,361]{0,1,2:T(8,128)S(1)}, s32[128,8,361]{0,1,2:T(8,128)}, u32[]{:S(2)}) copy-start(s32[128,8,361]{0,1,2:T(8,128)} %param.14) | copy-start | bytes 4435972
  160.0 0.7 copy-start.5
  161.3 46.1 %copy-start.1 = (bf16[128,11552]{0,1:T(8,128)(2,1)S(1)}, bf16[128,11552]{0,1:T(8,128)(2,1)}, u32[]{:S(2)}) copy-start(bf16[128,11552]{0,1:T(8,128)(2,1)} %param.11) | copy-start | bytes 8871940
  161.8 2.6 %copy-start.10 = (bf16[256]{0:T(256)(128)(2,1)S(1)}, bf16[256]{0:T(256)(128)(2,1)}, u32[]{:S(2)}) copy-start(bf16[256]{0:T(256)(128)(2,1)} %param.20) | copy-start | bytes 1540
  161.8 2.6 %copy-start.4 = (f32[128,256]{1,0:T(8,128)S(1)}, f32[128,256]{1,0:T(8,128)}, u32[]{:S(2)}) copy-start(f32[128,256]{1,0:T(8,128)} %copy-done.3) | copy-start | bytes 393220
  161.8 2.7 %copy-start.11 = (s32[128]{0:T(128)S(1)}, s32[128]{0:T(128)}, u32[]{:S(2)}) copy-start(s32[128]{0:T(128)} %param.13) | copy-start | bytes 1540
  164.6 42.8 %copy-start.8 = (f32[128]{0:T(128)}, f32[128]{0:T(128)S(1)}, u32[]{:S(2)}) copy-start(f32[128]{0:T(128)S(1)} %fusion.10) | copy-start | bytes 1540
where the time goes:
time: 208 us; the launch traced here: 207 us
  matrix products  145 us (70%)
  blocking collectives  42 us (20%)
  other arithmetic  15.1 us (7%)
  local copies, waits for them, and re-layouts  3.4 us (2%)
    conv_general_dilated x3, matrix products, convolve(): lax.conv_general_dilated(inputs, kernel, (1, 1), 'SAME', dimension_number...  139 us
    unnamed x1, blocking collectives  42 us
    reduce_sum x1, other arithmetic, evaluate(): pooled = jnp.mean(hidden, axis=(1, 2), dtype=jnp.float32)  12.1 us
    dot_general x1, matrix products, evaluate(): jnp.einsum('bhwc,cf->bfhw', hidden, policy_weight, preferred_element_type...  6.2 us

commit v1 on v0

--- a/solution.py
+++ b/solution.py
@@ -80,7 +80,11 @@
         jnp.float32
     )
     partial_sums = jnp.dot(leaf_values, onehot, precision=lax.Precision.HIGHEST)
-    tree_value = lax.psum_scatter(partial_sums, ("search", "net"), scatter_dimension=0, tiled=True)
+    groups = lax.axis_size(("search", "net"))
+    spread = lax.all_to_all(
+        partial_sums.reshape(groups, TREE_DEV), ("search", "net"), 0, 0, tiled=True
+    )
+    tree_value = jnp.sum(spread, axis=0)
     return (priors, leaf_values, tree_value)
 
 

time: 208 us -> 202 us (0.971)
  blocking collectives: 42 us -> 0 us
  matrix products: 145 us -> 161 us
  other arithmetic: 15.1 us -> 29.1 us
  starting transfers between devices: 0 us -> 7.33 us
    unnamed x1 -> x0, blocking collectives: 42 us -> none
    reduce_sum x1, other arithmetic: 12.1 us -> 25.6 us  [evaluate(): pooled = jnp.mean(hidden, axis=(1, 2), dtype=jnp.float32)]
    conv_general_dilated x3, matrix products: 139 us -> 150 us  [convolve(): lax.conv_general_dilated(inputs, kernel, (1, 1), 'SAME', dimension_number...]
    all_to_all x0 -> x1, starting transfers between devices: none -> 7.33 us  [body(): lax.all_to_all(partial_sums.reshape(groups, TREE_DEV), ('search', 'net'),...]
    dot_general x1, matrix products: 6.2 us -> 11 us  [evaluate(): jnp.einsum('bhwc,cf->bfhw', hidden, policy_weight, preferred_element_type...]
  transfers between devices with their start and end apart: 0 -> 1, of which waited for: 0 -> 0; matrix products, arithmetic and copies ran while one was open for 0% -> 7% of each run, Pallas kernels for 0% -> 0%
where the time goes in v1:
time: 202 us
  matrix products  161 us (80%)
  other arithmetic  29.1 us (14%)
  starting transfers between devices  7.33 us (4%)
  local copies, waits for them, and re-layouts  2.63 us (1%)
    conv_general_dilated x3, matrix products, convolve(): lax.conv_general_dilated(inputs, kernel, (1, 1), 'SAME', dimension_number...  150 us
    reduce_sum x1, other arithmetic, evaluate(): pooled = jnp.mean(hidden, axis=(1, 2), dtype=jnp.float32)  25.6 us
    dot_general x1, matrix products, evaluate(): jnp.einsum('bhwc,cf->bfhw', hidden, policy_weight, preferred_element_type...  11 us
    all_to_all x1, starting transfers between devices, body(): lax.all_to_all(partial_sums.reshape(groups, TREE_DEV), ('search', 'net'),...  7.33 us
  transfers between devices with their start and end apart: 1, of which 0 were waited for; matrix products, arithmetic and copies ran while one was open for 7% of the time, Pallas kernels for 0%

profile of v1, /device:TPU:0, one launch (start us, length us, event | category | flops | bytes accessed | tf_op | source)
XLA Modules:
  0.0 201.9 jit_solution(15842366170903341018)
XLA Ops:
  0.6 0.0 copy-start
  0.6 1.8 copy-done
  2.5 17.2 %maximum_convert_fusion.2 = bf16[128,19,19,256]{3,0,2,1:T(8,128)(2,1)} fusion(bf16[128,19,19,32]{0,3,2,1:T(8,128)(2,1)S(1)} %bitcast.45, bf16[3,3,32,256]{3,2,1,0:T(8,128)(2,1)} %param.15), kind=kOutput, calls=%fused_computation.3 | convolution fusion | flops 6367543296 | bytes 26763264 | tf_op jit(solution)/shard_map/conv_general_dilated | solution.py:14
  19.6 68.8 %fusion.4 = bf16[128,19,19,256]{3,0,2,1:T(8,128)(2,1)} fusion(bf16[128,19,19,256]{3,0,2,1:T(8,128)(2,1)} %maximum_convert_fusion.2, bf16[1,3,3,256,256]{4,3,2,1,0:T(8,128)(2,1)} %param.16), kind=kOutput, calls=%fused_computation.13 | convolution fusion | flops 50751078400 | bytes 48496640 | tf_op jit(solution)/shard_map/conv_general_dilated | solution.py:14
  88.4 0.0 copy-start.9
  88.4 0.0 copy-start.2
  88.4 0.0 copy-start.8
  88.4 25.6 %maximum_convert_fusion.5.clone.4 = bf16[128,19,19,256]{3,0,2,1:T(8,128)(2,1)} fusion(bf16[128,19,19,256]{3,0,2,1:T(8,128)(2,1)} %fusion.4), kind=kLoop, calls=%fused_computation.2.clone.clone.clone.clone.clone.clone.1 | loop fusion | flops 35487744 | bytes 47316992 | tf_op jit(solution)/shard_map/reduce_sum | solution.py:35
  114.6 0.0 copy-done.9
  114.7 0.0 copy-done.2
  114.7 0.0 copy-done.8
  114.7 0.0 copy-start.10
  114.7 0.0 copy-start.6
  114.7 0.0 copy-start.3
  114.7 63.9 %convert_reduce_fusion = (f32[128,256]{1,0:T(8,128)S(1)}, bf16[128,19,19,256]{3,0,2,1:T(8,128)(2,1)}) fusion(bf16[1,3,3,256,256]{4,3,2,1,0:T(8,128)(2,1)S(1)} %copy-done.8, bf16[128,19,19,256]{3,0,2,1:T(8,128)(2,1)S(1)} %copy-done.2, bf16[128,19,19,256]{3,0,2,1:T(8,128)(2,1)} %maximum_convert_fusion.5.clone.4), kind=kOutput, calls=%fused_computation | convolution fusion | flops 50822021120 | bytes 72286208 | tf_op jit(solution)/shard_map/conv_general_dilated | solution.py:14
  178.6 0.0 copy-start.5
  178.6 0.2 fusion.10
  178.8 0.0 copy-done.10
  178.8 0.0 copy-start.7
  178.8 0.2 fusion.11
  179.0 0.7 all_to_all.6
  179.7 7.3 %all-to-all-start = ((f32[32,1,8]{2,1,0:T(1,128)}), f32[32,1,8]{2,1,0:T(1,128)S(1)}, u32[]{:S(2)}, u32[]{:S(2)}) async-start(f32[32,1,8]{2,1,0:T(1,128)} %bitcast.12), calls=%async_computation | async-start | bytes 32768 | tf_op jit(solution)/shard_map/all_to_all | solution.py:84
  187.1 0.0 copy-done.6
  187.1 0.2 fusion.6
  187.3 0.0 copy-done.3
  187.3 0.2 broadcast_compare_fusion
  187.5 0.0 copy-done.5
  187.5 0.0 copy-start.4
  187.5 11.0 %convolution_convert_fusion = bf16[128,19,19,8]{0,3,2,1:T(8,128)(2,1)S(1)} fusion(bf16[128,19,19,256]{3,0,2,1:T(8,128)(2,1)} %get-tuple-element.4, bf16[256,8]{0,1:T(8,128)(2,1)S(1)} %copy-done.5), kind=kOutput, calls=%fused_computation.10 | convolution fusion | flops 189637632 | bytes 24401920 | tf_op jit(solution)/shard_map/bhwc,cf->bfhw/dot_general | solution.py:32
  198.5 0.0 copy-done.7
  198.5 0.0 copy-done.4
  198.5 0.6 select_reduce_fusion
  199.1 0.0 copy-start.1
  199.1 0.5 fusion.2
  199.6 1.7 divide_multiply_fusion
  201.3 0.0 all-to-all-done
  201.3 0.6 reduce_sum.29
  201.9 0.0 copy-done.1
  (2 shorter events, 0.0 us)
Async XLA Ops:
  0.6 1.8 copy-start
  88.4 26.2 %copy-start.9 = (bf16[256]{0:T(256)(128)(2,1)S(1)}, bf16[256]{0:T(256)(128)(2,1)}, u32[]{:S(2)}) copy-start(bf16[256]{0:T(256)(128)(2,1)} %param.20) | copy-start | bytes 1540
  88.4 26.2 %copy-start.2 = (bf16[128,19,19,256]{3,0,2,1:T(8,128)(2,1)S(1)}, bf16[128,19,19,256]{3,0,2,1:T(8,128)(2,1)}, u32[]{:S(2)}) copy-start(bf16[128,19,19,256]{3,0,2,1:T(8,128)(2,1)} %maximum_convert_fusion.2) | copy-start | bytes 70975488
  88.4 26.2 %copy-start.8 = (bf16[1,3,3,256,256]{4,3,2,1,0:T(8,128)(2,1)S(1)}, bf16[1,3,3,256,256]{4,3,2,1,0:T(8,128)(2,1)}, u32[]{:S(2)}) copy-start(bf16[1,3,3,256,256]{4,3,2,1,0:T(8,128)(2,1)} %param.17) | copy-start | bytes 3538948
  114.7 64.1 %copy-start.10 = (s32[128]{0:T(128)S(1)}, s32[128]{0:T(128)}, u32[]{:S(2)}) copy-start(s32[128]{0:T(128)} %param.13) | copy-start | bytes 1540
  114.7 72.4 %copy-start.6 = (bf16[256,8]{0,1:T(8,128)(2,1)S(1)}, bf16[256,8]{0,1:T(8,128)(2,1)}, u32[]{:S(2)}) copy-start(bf16[256,8]{0,1:T(8,128)(2,1)} %param.19) | copy-start | bytes 12292
  114.7 72.5 %copy-start.3 = (s32[128,8,361]{0,1,2:T(8,128)S(1)}, s32[128,8,361]{0,1,2:T(8,128)}, u32[]{:S(2)}) copy-start(s32[128,8,361]{0,1,2:T(8,128)} %param.14) | copy-start | bytes 4435972
  178.6 8.9 %copy-start.5 = (bf16[256,8]{0,1:T(8,128)(2,1)S(1)}, bf16[256,8]{0,1:T(8,128)(2,1)}, u32[]{:S(2)}) copy-start(bf16[256,8]{0,1:T(8,128)(2,1)} %param.18) | copy-start | bytes 12292
  178.8 19.7 %copy-start.7 = (f32[128]{0:T(128)}, f32[128]{0:T(128)S(1)}, u32[]{:S(2)}) copy-start(f32[128]{0:T(128)S(1)} %fusion.10) | copy-start | bytes 1540
  179.7 21.6 %all-to-all-start = ((f32[32,1,8]{2,1,0:T(1,128)}), f32[32,1,8]{2,1,0:T(1,128)S(1)}, u32[]{:S(2)}, u32[]{:S(2)}) async-start(f32[32,1,8]{2,1,0:T(1,128)} %bitcast.12), calls=%async_computation | async-start | bytes 32768 | tf_op jit(solution)/shard_map/all_to_all | solution.py:84
  187.5 11.0 %copy-start.4 = (f32[8]{0:T(128)S(1)}, f32[8]{0:T(128)}, u32[]{:S(2)}) copy-start(f32[8]{0:T(128)} %param.21) | copy-start | bytes 100
  199.1 2.8 %copy-start.1 = (bf16[128,11552]{0,1:T(8,128)(2,1)S(1)}, bf16[128,11552]{0,1:T(8,128)(2,1)}, u32[]{:S(2)}) copy-start(bf16[128,11552]{0,1:T(8,128)(2,1)} %param.11) | copy-start | bytes 8871940

commit v2 on v0

--- a/solution.py
+++ b/solution.py
@@ -1,13 +1,23 @@
+import functools
+
 import jax
 import jax.numpy as jnp
 from jax import lax
+from jax.experimental import pallas as pl
+from jax.experimental.pallas import tpu as pltpu
 from jax.sharding import PartitionSpec as P
 
 SIDE = 19
 BOARD = 361
+MOVES = 362
 PLANES = 32
 FACT = 8
 TREE_DEV = 8
+AXES = ("search", "net")
+CHUNK = 8
+PASSES = 3
+CORE_CAP = 64
+LINK_CAP = 24
 
 
 def convolve(inputs, kernel):
@@ -49,6 +59,44 @@
     peak = jnp.max(jnp.where(allowed, scaled, -1e30), axis=2, keepdims=True)
     weights = jnp.exp(jnp.where(allowed, scaled - peak, -1e30))
     return weights / jnp.sum(weights, axis=2, keepdims=True)
+
+
+def plan_kernel(masks, caps, counts_ref, out_ref):
+    counts_all = counts_ref[...]
+    lanes = counts_all.shape[1]
+    lane = lax.broadcasted_iota(jnp.int32, counts_all.shape, 1)
+
+    def swap(x, mask):
+        up = pltpu.roll(x, mask, 1)
+        up_from = pltpu.roll(lane, mask, 1)
+        down = pltpu.roll(x, lanes - mask, 1)
+        return jnp.where(up_from == (lane ^ mask), up, down)
+
+    flows = [jnp.zeros_like(counts_all) for _ in masks]
+    for _ in range(PASSES):
+        for e, (mask, cap) in enumerate(zip(masks, caps)):
+            sent = sum(flows)
+            got = sum(swap(f, m) for f, m in zip(flows, masks))
+            load = counts_all - sent + got
+            own = counts_all - sent
+            move = jnp.right_shift(jnp.maximum(load - swap(load, mask), 0), 1)
+            cancel = jnp.minimum(move, swap(flows[e], mask))
+            add = jnp.clip(move - cancel, 0, jnp.minimum(cap - flows[e], own))
+            flows[e] = flows[e] + add - swap(cancel, mask)
+    rows = flows + [swap(f, m) for f, m in zip(flows, masks)]
+    rows = rows + [jnp.zeros_like(counts_all)] * (out_ref.shape[0] - len(rows))
+    out_ref[...] = jnp.concatenate(rows, axis=0)
+
+
+def make_plan(counts_all, masks, caps):
+    groups = counts_all.shape[0]
+    lanes = -(-groups // 128) * 128
+    padded = jnp.zeros((1, lanes), jnp.int32).at[0, :groups].set(counts_all)
+    rows = -(-2 * len(masks) // 8) * 8
+    return pl.pallas_call(
+        functools.partial(plan_kernel, masks, caps),
+        out_shape=jax.ShapeDtypeStruct((rows, lanes), jnp.int32),
+    )(padded)
 
 
 def body(
@@ -64,39 +112,143 @@
     value_weight,
     logit_scale,
 ):
-    slot_count = states.shape[0]
+    weights = (in_weight, mid_weight, out_weight, policy_weight, pass_weight, value_weight)
+    slot_count, row = states.shape
+    groups = lax.axis_size(AXES)
+    net_size = lax.axis_size("net")
+    me = lax.axis_index(AXES)
     own_count = counts[0]
-    slot_index = jnp.arange(slot_count, dtype=jnp.int32)
-    returned_logits, returned_values = evaluate(
-        states, in_weight, mid_weight, out_weight, policy_weight, pass_weight, value_weight
-    )
-    alive = slot_index < own_count
-    priors = masked_priors(returned_logits, legal, logit_scale) * alive[:, None, None].astype(
-        jnp.float32
-    )
-    leaf_values = jnp.where(alive, returned_values.astype(jnp.float32), 0.0)
-    tree_total = TREE_DEV * lax.axis_size(("search", "net"))
+
+    counts_all = lax.all_to_all(
+        jnp.broadcast_to(counts, (groups, 1)), AXES, 0, 0, tiled=True
+    ).reshape(groups)
+
+    masks = (4, 2, 2 * net_size, 1, net_size)
+    caps = (LINK_CAP, LINK_CAP, LINK_CAP, LINK_CAP, CORE_CAP)
+    plan = make_plan(counts_all, masks, caps)
+    mine = lax.dynamic_slice(plan, (0, me), (plan.shape[0], 1))
+    send = [mine[e, 0] for e in range(len(masks))]
+    recv = [mine[len(masks) + e, 0] for e in range(len(masks))]
+    keep = own_count - sum(send)
+
+    starts = []
+    offset = keep
+    for e in range(len(masks)):
+        starts.append(offset)
+        offset = offset + send[e]
+    pairs = [[(d, d ^ m) for d in range(groups)] for m in masks]
+    incoming = []
+    for e, cap in enumerate(caps):
+        idx = jnp.clip(starts[e] + jnp.arange(cap, dtype=jnp.int32), 0, slot_count - 1)
+        outgoing = jnp.take(states, idx, axis=0)
+        incoming.append(lax.ppermute(outgoing, AXES, pairs[e]))
+
+    full = keep // CHUNK
+    rem = keep - full * CHUNK
+
+    def own_step(t, carry):
+        logits_acc, values_acc = carry
+        rows = lax.dynamic_slice(states, (t * CHUNK, 0), (CHUNK, row))
+        logits, values = evaluate(rows, *weights)
+        logits_acc = lax.dynamic_update_slice(logits_acc, logits, (t * CHUNK, 0, 0))
+        values_acc = lax.dynamic_update_slice(values_acc, values, (t * CHUNK,))
+        return logits_acc, values_acc
+
+    own_logits, own_values = lax.fori_loop(
+        0,
+        full,
+        own_step,
+        (
+            jnp.zeros((slot_count, FACT, MOVES), jnp.bfloat16),
+            jnp.zeros((slot_count,), jnp.bfloat16),
+        ),
+    )
+
+    tail_idx = jnp.clip(full * CHUNK + jnp.arange(CHUNK, dtype=jnp.int32), 0, slot_count - 1)
+    pool = jnp.concatenate([jnp.take(states, tail_idx, axis=0)] + incoming, axis=0)
+    pool_rows = pool.shape[0]
+    work_rows = -(-pool_rows // CHUNK) * CHUNK
+    k = jnp.arange(work_rows, dtype=jnp.int32)
+    work_idx = jnp.where(k < rem, k, 0)
+    seg_start = rem
+    base = CHUNK
+    recv_pos = []
+    for e, cap in enumerate(caps):
+        inside = (k >= seg_start) & (k < seg_start + recv[e])
+        work_idx = jnp.where(inside, base + k - seg_start, work_idx)
+        recv_pos.append(seg_start)
+        seg_start = seg_start + recv[e]
+        base = base + cap
+    work_count = seg_start
+    work_idx = jnp.clip(work_idx, 0, pool_rows - 1)
+
+    def work_step(t, carry):
+        logits_acc, values_acc = carry
+        idx = lax.dynamic_slice(work_idx, (t * CHUNK,), (CHUNK,))
+        rows = jnp.take(pool, idx, axis=0)
+        logits, values = evaluate(rows, *weights)
+        logits_acc = lax.dynamic_update_slice(logits_acc, logits, (t * CHUNK, 0, 0))
+        values_acc = lax.dynamic_update_slice(values_acc, values, (t * CHUNK,))
+        return logits_acc, values_acc
+
+    work_logits, work_values = lax.fori_loop(
+        0,
+        (work_count + CHUNK - 1) // CHUNK,
+        work_step,
+        (
+            jnp.zeros((work_rows, FACT, MOVES), jnp.bfloat16),
+            jnp.zeros((work_rows,), jnp.bfloat16),
+        ),
+    )
+
+    back_logits = []
+    back_values = []
+    for e, cap in enumerate(caps):
+        idx = jnp.clip(recv_pos[e] + jnp.arange(cap, dtype=jnp.int32), 0, work_rows - 1)
+        back_logits.append(lax.ppermute(jnp.take(work_logits, idx, axis=0), AXES, pairs[e]))
+        back_values.append(lax.ppermute(jnp.take(work_values, idx, axis=0), AXES, pairs[e]))
+
+    all_logits = jnp.concatenate([own_logits, work_logits] + back_logits, axis=0)
+    all_values = jnp.concatenate([own_values, work_values] + back_values, axis=0)
+    slot = jnp.arange(slot_count, dtype=jnp.int32)
+    pick = jnp.where(slot < full * CHUNK, slot, slot_count + slot - full * CHUNK)
+    base = slot_count + work_rows
+    for e, cap in enumerate(caps):
+        inside = (slot >= starts[e]) & (slot < starts[e] + send[e])
+        pick = jnp.where(inside, base + slot - starts[e], pick)
+        base = base + cap
+    pick = jnp.clip(pick, 0, all_logits.shape[0] - 1)
+    slot_logits = jnp.take(all_logits, pick, axis=0)
+    slot_values = jnp.take(all_values, pick, axis=0)
+
+    alive = slot < own_count
+    priors = jnp.where(
+        alive[:, None, None], masked_priors(slot_logits, legal, logit_scale), 0.0
+    )
+    leaf_values = jnp.where(alive, slot_values.astype(jnp.float32), 0.0)
+    tree_total = TREE_DEV * groups
     onehot = (owners[:, None] == jnp.arange(tree_total, dtype=jnp.int32)[None, :]).astype(
         jnp.float32
     )
     partial_sums = jnp.dot(leaf_values, onehot, precision=lax.Precision.HIGHEST)
-    tree_value = lax.psum_scatter(partial_sums, ("search", "net"), scatter_dimension=0, tiled=True)
+    spread = lax.all_to_all(partial_sums.reshape(groups, TREE_DEV), AXES, 0, 0, tiled=True)
+    tree_value = jnp.sum(spread, axis=0)
     return (priors, leaf_values, tree_value)
 
 
 def solution(mesh):
     in_specs = (
-        P(("search", "net"), None),
-        P(("search", "net")),
-        P(("search", "net")),
-        P(("search", "net"), None, None),
-        P(),
-        P(),
-        P(),
-        P(),
-        P(),
-        P(),
-        P(),
-    )
-    out_specs = (P(("search", "net"), None, None), P(("search", "net")), P(("search", "net")))
+        P(AXES, None),
+        P(AXES),
+        P(AXES),
+        P(AXES, None, None),
+        P(),
+        P(),
+        P(),
+        P(),
+        P(),
+        P(),
+        P(),
+    )
+    out_specs = (P(AXES, None, None), P(AXES), P(AXES))
     return jax.shard_map(body, mesh=mesh, in_specs=in_specs, out_specs=out_specs, check_vma=False)

time: 208 us -> 305 us (1.47); the launches traced: 207 us -> 299 us
  starting transfers between devices: 0 us -> 68.9 us
  local copies, waits for them, and re-layouts: 3.4 us -> 64.2 us
  matrix products: 145 us -> 93.8 us
  blocking collectives: 42 us -> 0 us
  other arithmetic: 15.1 us -> 35.6 us
  loops' own time: 0 us -> 13.5 us
  between operations: 1.62 us -> 11.7 us
  waiting for transfers between devices: 0 us -> 6.63 us
  Pallas kernels: 0 us -> 4.49 us
    conv_general_dilated x3 -> x8, matrix products: 139 us -> 77.8 us  [convolve(): lax.conv_general_dilated(inputs, kernel, (1, 1), 'SAME', dimension_number...]
    ppermute x0 -> x15, starting transfers between devices: none -> 58.3 us  [the longest x5 44.7 us: body(): lax.ppermute(jnp.take(work_values, idx, axis=0), AXES, pairs[e])]
    unnamed x1 -> x0, blocking collectives: 42 us -> none
    gather x0 -> x27, local copies, waits for them, and re-layouts: none -> 36.4 us  [the longest x8 16.7 us: work_step(): rows = jnp.take(pool, idx, axis=0)]
    select_n x0 -> x33, other arithmetic: none -> 17.1 us  [the longest x10 11.3 us: body(): outgoing = jnp.take(states, idx, axis=0)]
    another operation x0 -> x2, loops' own time: none -> 13.5 us  [the longest x1 13 us: body(): lax.fori_loop(0, full, own_step, (jnp.zeros((slot_count, FACT, MOVES), jn...]
    reduce_sum x1, other arithmetic: 12.1 us -> 0.56 us  [body(): tree_value = jnp.sum(spread, axis=0)]
    all_to_all x0 -> x2, starting transfers between devices: none -> 10.5 us  [the longest x1 7.33 us: body(): lax.all_to_all(jnp.broadcast_to(counts, (groups, 1)), AXES, 0, 0, tiled=T...]
  transfers between devices with their start and end apart: 0 -> 17, of which waited for: 0 -> 1; matrix products, arithmetic and copies ran while one was open for 0% -> 15% of each run, Pallas kernels for 0% -> 0%
where the time goes in v2:
time: 305 us; the launch traced here: 299 us
  matrix products  93.8 us (31%)
  starting transfers between devices  68.9 us (23%)
  local copies, waits for them, and re-layouts  64.2 us (21%)
  other arithmetic  35.6 us (12%)
  loops' own time  13.5 us (4%)
  between operations  11.7 us (4%)
  waiting for transfers between devices  6.63 us (2%)
  Pallas kernels  4.49 us (1%)
    conv_general_dilated x8, matrix products, convolve(): lax.conv_general_dilated(inputs, kernel, (1, 1), 'SAME', dimension_number...  77.8 us
    ppermute x5, starting transfers between devices, body(): lax.ppermute(jnp.take(work_values, idx, axis=0), AXES, pairs[e])  44.7 us
    gather x8, local copies, waits for them, and re-layouts, work_step(): rows = jnp.take(pool, idx, axis=0)  16.7 us
    unnamed x52, local copies, waits for them, and re-layouts  13.6 us
    dot_general x4, matrix products, evaluate(): jnp.einsum('bhwc,cf->bfhw', hidden, policy_weight, preferred_element_type...  13.4 us
    another operation x1, loops' own time, body(): lax.fori_loop(0, full, own_step, (jnp.zeros((slot_count, FACT, MOVES), jn...  13 us
    select_n x10, other arithmetic, body(): outgoing = jnp.take(states, idx, axis=0)  11.3 us
    all_to_all x1, starting transfers between devices, body(): lax.all_to_all(jnp.broadcast_to(counts, (groups, 1)), AXES, 0, 0, tiled=T...  7.33 us
  transfers between devices with their start and end apart: 17, of which 1 were waited for; matrix products, arithmetic and copies ran while one was open for 15% of the time, Pallas kernels for 0%

profile of v2, /device:TPU:0, one launch (start us, length us, event | category | flops | bytes accessed | tf_op | source)
XLA Modules:
  0.0 298.8 jit_solution(4846420531869785023)
XLA Ops:
  1.9 7.3 %all-to-all-start = ((s32[32,1,1]{2,1,0:T(1,128)}), s32[32,1,1]{2,1,0:T(1,128)S(1)}, u32[]{:S(2)}, u32[]{:S(2)}) async-start(s32[32,1,1]{2,1,0:T(1,128)} %broadcast_in_dim.140), calls=%async_computation | async-start | bytes 32768 | tf_op jit(solution)/shard_map/all_to_all | solution.py:122
  9.8 2.3 broadcast_compare_fusion
  12.7 3.4 %copy.88 = bf16[128,11552]{1,0:T(8,128)(2,1)S(1)} copy(bf16[128,11552]{0,1:T(8,128)(2,1)} %param.23) | data formatting | bytes 5914624 | tf_op jit(solution)/shard_map/while | solution.py:157
  16.7 1.3 fusion.36
  18.5 4.5 %shard_map.130 = s32[16,128]{1,0:T(8,128)} custom-call(s32[1,128]{1,0:T(1,128)} %scatter.4.counts_ref), custom_call_target="tpu_custom_call" | custom-call | tf_op jit(solution)/shard_map/pallas_call | solution.py:96
  23.0 1.7 fusion.47
  44.9 1.3 gather_fusion.1
  46.3 0.9 gather_fusion.7
  47.2 1.6 broadcast_select_fusion.6
  48.8 2.7 collective-permute-start
  52.1 0.9 gather_fusion.8
  53.0 1.6 broadcast_select_fusion.5
  54.6 1.5 collective-permute-start.1
  56.7 0.9 gather_fusion.9
  57.6 1.6 broadcast_select_fusion.4
  59.2 1.5 collective-permute-start.2
  61.4 0.9 gather_fusion.10
  62.4 1.5 broadcast_select_fusion.3
  63.9 1.5 collective-permute-start.3
  65.4 1.3 pad_clamp_fusion.2
  66.7 2.7 gather_fusion.2
  69.4 2.8 broadcast_select_fusion.1
  73.4 1.0 broadcast_in_dim.142
  74.4 13.0 %while.25 = (s32[]{:T(128)}, bf16[128,8,362]{2,1,0:T(8,128)(2,1)}, bf16[128]{0:T(256)(128)(2,1)S(1)}, s32[]{:T(128)}, bf16[128,11552]{1,0:T(8,128)(2,1)S(1)}, /*...) while((s32[]{:T(128)}, bf16[128,8,362]{2,1,0:T(8,128)(2,1)}, ...), condition=%wide.region_3.4_spmd, body=%wide.region_1.3_spmd.sunk | while | flops 6759939072 | bytes 9614583 | solution.py:157
  88.3 2.1 constant_dynamic-update-slice_fusion.11
  90.4 1.9 constant_dynamic-update-slice_fusion.4
  92.3 1.9 constant_dynamic-update-slice_fusion.3
  94.3 1.9 constant_dynamic-update-slice_fusion.2
  96.2 1.9 constant_dynamic-update-slice_fusion.1
  98.1 2.6 constant_dynamic-update-slice_fusion
  100.8 114.0 %while.26 = (s32[]{:T(128)}, bf16[168,8,362]{2,1,0:T(8,128)(2,1)S(1)}, bf16[168]{0:T(256)(128)(2,1)S(1)}, s32[]{:T(128)}, s32[168]{0:T(256)S(1)}, /*index=5*/bf1...) while((s32[]{:T(128)}, ...), condition=%wide.region_6.8_spmd, body=%wide.region_4.7_spmd.sunk | while | flops 6760032768 | bytes 10007695 | solution.py:194
  100.9 3.4 %gather_fusion = bf16[8,11552]{1,0:T(8,128)(2,1)S(1)} fusion(bf16[168,11552]{1,0:T(8,128)(2,1)} %get-tuple-element.500, s32[1024]{0:T(1024)S(1)} %pad_clamp_fusion.14), kind=kCustom, calls=%fused_computation.1.clone.1 | custom fusion | bytes 369696 | tf_op jit(solution)/shard_map/while/body/jit(_take)/gather | solution.py:188
  105.3 3.0 %maximum_convert_fusion.9 = bf16[8,19,19,256]{3,0,2,1:T(8,128)(2,1)} fusion(bf16[3,3,32,256]{3,2,1,0:T(8,128)(2,1)S(1)} %get-tuple-element.501, bf16[8,19,19,32]{3,2,1,0:T(8,128)(2,1)S(1)} %broadcast_select_fusion.19), kind=kOutput, calls=%fused_computation.45.clone.1 | convolution fusion | flops 397971456 | bytes 1810944 | tf_op jit(solution)/shard_map/while/body/conv_general_dilated | solution.py:24
  108.3 16.4 %convert_reduce_fusion.5 = (f32[8,256]{1,0:T(8,128)S(1)}, bf16[8,19,19,256]{3,0,2,1:T(8,128)(2,1)S(1)}) fusion(bf16[1,3,3,256,256]{4,3,2,1,0:T(8,128)(2,1)} %get-tuple-element.503, bf16[8,19,19,256]{3,0,2,1:T(8,128)(2,1)} %maximum_convert_fusion.9, bf16[1,3,3,256,256]{4,3,2,1,0:T(8,128)(2,1)} %get-tuple-element.502), kind=kOutput, calls=%fused_computation.42.clone.1 | convolution fusion | flops 6349797376 | bytes 5324800 | tf_op jit(solution)/shard_map/while/body/conv_general_dilated | solution.py:24
  125.0 3.3 %convolution_convert_fusion.7 = bf16[8,19,19,8]{0,3,2,1:T(8,128)(2,1)S(1)} fusion(bf16[8,19,19,256]{3,0,2,1:T(8,128)(2,1)S(1)} %get-tuple-element.417, bf16[256,8]{0,1:T(8,128)(2,1)S(1)} %get-tuple-element.504), kind=kOutput, calls=%fused_computation.46.clone.1 | convolution fusion | flops 11852352 | bytes 1528960 | tf_op jit(solution)/shard_map/while/body/bhwc,cf->bfhw/dot_general | solution.py:42
  129.4 3.4 %gather_fusion = bf16[8,11552]{1,0:T(8,128)(2,1)S(1)} fusion(bf16[168,11552]{1,0:T(8,128)(2,1)} %get-tuple-element.500, s32[1024]{0:T(1024)S(1)} %pad_clamp_fusion.14), kind=kCustom, calls=%fused_computation.1.clone.1 | custom fusion | bytes 369696 | tf_op jit(solution)/shard_map/while/body/jit(_take)/gather | solution.py:188
  133.7 3.0 %maximum_convert_fusion.9 = bf16[8,19,19,256]{3,0,2,1:T(8,128)(2,1)} fusion(bf16[3,3,32,256]{3,2,1,0:T(8,128)(2,1)S(1)} %get-tuple-element.501, bf16[8,19,19,32]{3,2,1,0:T(8,128)(2,1)S(1)} %broadcast_select_fusion.19), kind=kOutput, calls=%fused_computation.45.clone.1 | convolution fusion | flops 397971456 | bytes 1810944 | tf_op jit(solution)/shard_map/while/body/conv_general_dilated | solution.py:24
  136.7 16.4 %convert_reduce_fusion.5 = (f32[8,256]{1,0:T(8,128)S(1)}, bf16[8,19,19,256]{3,0,2,1:T(8,128)(2,1)S(1)}) fusion(bf16[1,3,3,256,256]{4,3,2,1,0:T(8,128)(2,1)} %get-tuple-element.503, bf16[8,19,19,256]{3,0,2,1:T(8,128)(2,1)} %maximum_convert_fusion.9, bf16[1,3,3,256,256]{4,3,2,1,0:T(8,128)(2,1)} %get-tuple-element.502), kind=kOutput, calls=%fused_computation.42.clone.1 | convolution fusion | flops 6349797376 | bytes 5324800 | tf_op jit(solution)/shard_map/while/body/conv_general_dilated | solution.py:24
  153.5 3.3 %convolution_convert_fusion.7 = bf16[8,19,19,8]{0,3,2,1:T(8,128)(2,1)S(1)} fusion(bf16[8,19,19,256]{3,0,2,1:T(8,128)(2,1)S(1)} %get-tuple-element.417, bf16[256,8]{0,1:T(8,128)(2,1)S(1)} %get-tuple-element.504), kind=kOutput, calls=%fused_computation.46.clone.1 | convolution fusion | flops 11852352 | bytes 1528960 | tf_op jit(solution)/shard_map/while/body/bhwc,cf->bfhw/dot_general | solution.py:42
  157.8 3.4 %gather_fusion = bf16[8,11552]{1,0:T(8,128)(2,1)S(1)} fusion(bf16[168,11552]{1,0:T(8,128)(2,1)} %get-tuple-element.500, s32[1024]{0:T(1024)S(1)} %pad_clamp_fusion.14), kind=kCustom, calls=%fused_computation.1.clone.1 | custom fusion | bytes 369696 | tf_op jit(solution)/shard_map/while/body/jit(_take)/gather | solution.py:188
  162.2 3.0 %maximum_convert_fusion.9 = bf16[8,19,19,256]{3,0,2,1:T(8,128)(2,1)} fusion(bf16[3,3,32,256]{3,2,1,0:T(8,128)(2,1)S(1)} %get-tuple-element.501, bf16[8,19,19,32]{3,2,1,0:T(8,128)(2,1)S(1)} %broadcast_select_fusion.19), kind=kOutput, calls=%fused_computation.45.clone.1 | convolution fusion | flops 397971456 | bytes 1810944 | tf_op jit(solution)/shard_map/while/body/conv_general_dilated | solution.py:24
  165.2 16.4 %convert_reduce_fusion.5 = (f32[8,256]{1,0:T(8,128)S(1)}, bf16[8,19,19,256]{3,0,2,1:T(8,128)(2,1)S(1)}) fusion(bf16[1,3,3,256,256]{4,3,2,1,0:T(8,128)(2,1)} %get-tuple-element.503, bf16[8,19,19,256]{3,0,2,1:T(8,128)(2,1)} %maximum_convert_fusion.9, bf16[1,3,3,256,256]{4,3,2,1,0:T(8,128)(2,1)} %get-tuple-element.502), kind=kOutput, calls=%fused_computation.42.clone.1 | convolution fusion | flops 6349797376 | bytes 5324800 | tf_op jit(solution)/shard_map/while/body/conv_general_dilated | solution.py:24
  181.9 3.3 %convolution_convert_fusion.7 = bf16[8,19,19,8]{0,3,2,1:T(8,128)(2,1)S(1)} fusion(bf16[8,19,19,256]{3,0,2,1:T(8,128)(2,1)S(1)} %get-tuple-element.417, bf16[256,8]{0,1:T(8,128)(2,1)S(1)} %get-tuple-element.504), kind=kOutput, calls=%fused_computation.46.clone.1 | convolution fusion | flops 11852352 | bytes 1528960 | tf_op jit(solution)/shard_map/while/body/bhwc,cf->bfhw/dot_general | solution.py:42
  186.3 3.4 %gather_fusion = bf16[8,11552]{1,0:T(8,128)(2,1)S(1)} fusion(bf16[168,11552]{1,0:T(8,128)(2,1)} %get-tuple-element.500, s32[1024]{0:T(1024)S(1)} %pad_clamp_fusion.14), kind=kCustom, calls=%fused_computation.1.clone.1 | custom fusion | bytes 369696 | tf_op jit(solution)/shard_map/while/body/jit(_take)/gather | solution.py:188
  190.6 3.0 %maximum_convert_fusion.9 = bf16[8,19,19,256]{3,0,2,1:T(8,128)(2,1)} fusion(bf16[3,3,32,256]{3,2,1,0:T(8,128)(2,1)S(1)} %get-tuple-element.501, bf16[8,19,19,32]{3,2,1,0:T(8,128)(2,1)S(1)} %broadcast_select_fusion.19), kind=kOutput, calls=%fused_computation.45.clone.1 | convolution fusion | flops 397971456 | bytes 1810944 | tf_op jit(solution)/shard_map/while/body/conv_general_dilated | solution.py:24
  193.7 16.4 %convert_reduce_fusion.5 = (f32[8,256]{1,0:T(8,128)S(1)}, bf16[8,19,19,256]{3,0,2,1:T(8,128)(2,1)S(1)}) fusion(bf16[1,3,3,256,256]{4,3,2,1,0:T(8,128)(2,1)} %get-tuple-element.503, bf16[8,19,19,256]{3,0,2,1:T(8,128)(2,1)} %maximum_convert_fusion.9, bf16[1,3,3,256,256]{4,3,2,1,0:T(8,128)(2,1)} %get-tuple-element.502), kind=kOutput, calls=%fused_computation.42.clone.1 | convolution fusion | flops 6349797376 | bytes 5324800 | tf_op jit(solution)/shard_map/while/body/conv_general_dilated | solution.py:24
  210.4 3.3 %convolution_convert_fusion.7 = bf16[8,19,19,8]{0,3,2,1:T(8,128)(2,1)S(1)} fusion(bf16[8,19,19,256]{3,0,2,1:T(8,128)(2,1)S(1)} %get-tuple-element.417, bf16[256,8]{0,1:T(8,128)(2,1)S(1)} %get-tuple-element.504), kind=kOutput, calls=%fused_computation.46.clone.1 | convolution fusion | flops 11852352 | bytes 1528960 | tf_op jit(solution)/shard_map/while/body/bhwc,cf->bfhw/dot_general | solution.py:42
  217.5 0.8 gather_fusion.17
  219.0 0.8 gather_fusion.18
  220.5 0.9 gather_fusion.5
  221.4 0.9 gather_fusion.3
  222.4 29.0 %collective-permute-start.14 = (bf16[64]{0:T(256)(128)(2,1)S(1)}, bf16[64]{0:T(256)(128)(2,1)S(1)}, u32[]{:S(2)}, u32[]{:S(2)}) collective-permute-start(bf16[64]{0:T(256)(128)(2,1)S(1)} %broadcast_select_fusion.17), channel_id=1, source_target_pairs={{0,8},{1,9},{2,10},{3,11},{4,12},{5,13},{6,14},{7,15},{8,0},{9,1},... | collective-permute-start | bytes 392 | tf_op jit(solution)/shard_map/ppermute | solution.py:209
  251.5 4.0 %collective-permute-start.12 = (bf16[24]{0:T(256)(128)(2,1)S(1)}, bf16[24]{0:T(256)(128)(2,1)S(1)}, u32[]{:S(2)}, u32[]{:S(2)}) collective-permute-start(bf16[24]{0:T(256)(128)(2,1)S(1)} %broadcast_select_fusion.14), channel_id=1, source_target_pairs={{0,16},{1,17},{2,18},{3,19},{4,20},{5,21},{6,22},{7,23},{8,24},{9,... | collective-permute-start | bytes 152 | tf_op jit(solution)/shard_map/ppermute | solution.py:209
  255.6 11.6 %collective-permute-start.10 = (bf16[24]{0:T(256)(128)(2,1)S(1)}, bf16[24]{0:T(256)(128)(2,1)S(1)}, u32[]{:S(2)}, u32[]{:S(2)}) collective-permute-start(bf16[24]{0:T(256)(128)(2,1)S(1)} %broadcast_select_fusion.16), channel_id=1, source_target_pairs={{0,4},{1,5},{2,6},{3,7},{4,0},{5,1},{6,2},{7,3},{8,12},{9,13},{10,... | collective-permute-start | bytes 152 | tf_op jit(solution)/shard_map/ppermute | solution.py:209
  267.2 1.1 constant_dynamic-update-slice_fusion.10
  268.8 1.7 collective-permute-start.5
  270.9 2.0 collective-permute-start.7
  272.9 2.0 collective-permute-start.8
  275.0 1.3 gather_fusion.6
  276.3 1.7 convolution_bitcast_fusion.2
  278.0 3.2 %all-to-all-start.1 = ((f32[32,1,8]{2,1,0:T(1,128)}), f32[32,1,8]{2,1,0:T(1,128)S(1)}, u32[]{:S(2)}, u32[]{:S(2)}) async-start(f32[32,1,8]{2,1,0:T(1,128)} %convolution_bitcast_fusion.2), calls=%async_computation.1 | async-start | bytes 32768 | tf_op jit(solution)/shard_map/all_to_all | solution.py:234
  281.7 6.6 %all-to-all-done.1 = f32[32,1,8]{2,1,0:T(1,128)S(1)} async-done(((f32[32,1,8]{2,1,0:T(1,128)}), f32[32,1,8]{2,1,0:T(1,128)S(1)}, u32[]{:S(2)}, u32[]{:S(2)}) %all-to-all-start.1) | async-done | bytes 1056 | tf_op jit(solution)/shard_map/all_to_all | solution.py:234
  292.3 2.6 gather_fusion.4
  296.8 1.7 divide_select_fusion
  (177 shorter events, 37.8 us)
Async XLA Ops:
  1.9 14.8 %all-to-all-start = ((s32[32,1,1]{2,1,0:T(1,128)}), s32[32,1,1]{2,1,0:T(1,128)S(1)}, u32[]{:S(2)}, u32[]{:S(2)}) async-start(s32[32,1,1]{2,1,0:T(1,128)} %broadcast_in_dim.140), calls=%async_computation | async-start | bytes 32768 | tf_op jit(solution)/shard_map/all_to_all | solution.py:122
  48.8 41.7 %collective-permute-start = (bf16[24,11552]{1,0:T(8,128)(2,1)}, bf16[24,11552]{1,0:T(8,128)(2,1)}, u32[]{:S(2)}, u32[]{:S(2)}) collective-permute-start(bf16[24,11552]{1,0:T(8,128)(2,1)} %broadcast_select_fusion.6), channel_id=1, source_target_pairs={{0,4},{1,5},{2,6},{3,7},{4,0},{5,1},{6,2},{7,3},{8,12},{9,13},{10,... | collective-permute-start | bytes 1663496 | tf_op jit(solution)/shard_map/ppermute | solution.py:144
  54.6 37.8 %collective-permute-start.1 = (bf16[24,11552]{1,0:T(8,128)(2,1)}, bf16[24,11552]{1,0:T(8,128)(2,1)}, u32[]{:S(2)}, u32[]{:S(2)}) collective-permute-start(bf16[24,11552]{1,0:T(8,128)(2,1)} %broadcast_select_fusion.5), channel_id=1, source_target_pairs={{0,2},{1,3},{2,0},{3,1},{4,6},{5,7},{6,4},{7,5},{8,10},{9,11},{10,... | collective-permute-start | bytes 1663496 | tf_op jit(solution)/shard_map/ppermute | solution.py:144
  59.2 35.0 %collective-permute-start.2 = (bf16[24,11552]{1,0:T(8,128)(2,1)}, bf16[24,11552]{1,0:T(8,128)(2,1)}, u32[]{:S(2)}, u32[]{:S(2)}) collective-permute-start(bf16[24,11552]{1,0:T(8,128)(2,1)} %broadcast_select_fusion.4), channel_id=1, source_target_pairs={{0,16},{1,17},{2,18},{3,19},{4,20},{5,21},{6,22},{7,23},{8,24},{9,... | collective-permute-start | bytes 1663496 | tf_op jit(solution)/shard_map/ppermute | solution.py:144
  63.9 32.3 %collective-permute-start.3 = (bf16[24,11552]{1,0:T(8,128)(2,1)}, bf16[24,11552]{1,0:T(8,128)(2,1)}, u32[]{:S(2)}, u32[]{:S(2)}) collective-permute-start(bf16[24,11552]{1,0:T(8,128)(2,1)} %broadcast_select_fusion.3), channel_id=1, source_target_pairs={{0,1},{1,0},{2,3},{3,2},{4,5},{5,4},{6,7},{7,6},{8,9},{9,8},{10,11... | collective-permute-start | bytes 1663496 | tf_op jit(solution)/shard_map/ppermute | solution.py:144
  66.7 2.7 copy-start.11
  69.3 2.9 copy-start.15
  69.3 3.5 %copy-start.14 = (s32[24]{0:T(128)S(1)}, s32[24]{0:T(128)}, u32[]{:S(2)}) copy-start(s32[24]{0:T(128)} %compare_select_fusion.2) | copy-start | bytes 292
  69.3 5.1 %copy-start.2 = (bf16[256,8]{0,1:T(8,128)(2,1)S(1)}, bf16[256,8]{0,1:T(8,128)(2,1)}, u32[]{:S(2)}) copy-start(bf16[256,8]{0,1:T(8,128)(2,1)} %param.30) | copy-start | bytes 12292
  69.3 5.0 %copy-start.3 = (bf16[256,8]{0,1:T(8,128)(2,1)S(1)}, bf16[256,8]{0,1:T(8,128)(2,1)}, u32[]{:S(2)}) copy-start(bf16[256,8]{0,1:T(8,128)(2,1)} %param.31) | copy-start | bytes 12292
  69.4 5.0 %copy-start.18 = (bf16[3,3,32,256]{3,2,1,0:T(8,128)(2,1)S(1)}, bf16[3,3,32,256]{3,2,1,0:T(8,128)(2,1)}, u32[]{:S(2)}) copy-start(bf16[3,3,32,256]{3,2,1,0:T(8,128)(2,1)} %param.27) | copy-start | bytes 442372
  69.4 5.0 %copy-start.19 = (bf16[256]{0:T(256)(128)(2,1)S(1)}, bf16[256]{0:T(256)(128)(2,1)}, u32[]{:S(2)}) copy-start(bf16[256]{0:T(256)(128)(2,1)} %param.32) | copy-start | bytes 1540
  72.2 25.9 %collective-permute-start.4 = (bf16[64,11552]{1,0:T(8,128)(2,1)}, bf16[64,11552]{1,0:T(8,128)(2,1)}, u32[]{:S(2)}, u32[]{:S(2)}) collective-permute-start(bf16[64,11552]{1,0:T(8,128)(2,1)} %broadcast_select_fusion.1), channel_id=1, source_target_pairs={{0,8},{1,9},{2,10},{3,11},{4,12},{5,13},{6,14},{7,15},{8,0},{9,1},... | collective-permute-start | bytes 4435976 | tf_op jit(solution)/shard_map/ppermute | solution.py:144
  74.4 13.1 %copy-start.1 = (bf16[8,11552]{1,0:T(8,128)(2,1)S(1)}, bf16[8,11552]{1,0:T(8,128)(2,1)}, u32[]{:S(2)}) copy-start(bf16[8,11552]{1,0:T(8,128)(2,1)} %gather_fusion.1) | copy-start | bytes 554500
  74.4 13.9 %copy-start.13 = (s32[24]{0:T(128)S(1)}, s32[24]{0:T(128)}, u32[]{:S(2)}) copy-start(s32[24]{0:T(128)} %compare_select_fusion.3) | copy-start | bytes 292
  74.4 13.9 %copy-start.12 = (s32[24]{0:T(128)S(1)}, s32[24]{0:T(128)}, u32[]{:S(2)}) copy-start(s32[24]{0:T(128)} %compare_select_fusion.4) | copy-start | bytes 292
  221.4 46.9 %copy-start.10 = (pred[24]{0:T(512)(128)(4,1)S(1)}, pred[24]{0:T(512)(128)(4,1)}, u32[]{:S(2)}) copy-start(pred[24]{0:T(512)(128)(4,1)} %compare_and_fusion.4) | copy-start | bytes 76
  221.4 47.0 %copy-start.9 = (pred[24]{0:T(512)(128)(4,1)S(1)}, pred[24]{0:T(512)(128)(4,1)}, u32[]{:S(2)}) copy-start(pred[24]{0:T(512)(128)(4,1)} %compare_and_fusion.3) | copy-start | bytes 76
  222.4 46.2 %copy-start.8 = (pred[24]{0:T(512)(128)(4,1)S(1)}, pred[24]{0:T(512)(128)(4,1)}, u32[]{:S(2)}) copy-start(pred[24]{0:T(512)(128)(4,1)} %compare_and_fusion.2) | copy-start | bytes 76
  222.4 46.3 %copy-start.7 = (pred[24]{0:T(512)(128)(4,1)S(1)}, pred[24]{0:T(512)(128)(4,1)}, u32[]{:S(2)}) copy-start(pred[24]{0:T(512)(128)(4,1)} %compare_and_fusion.1) | copy-start | bytes 76
  222.4 52.5 %collective-permute-start.14 = (bf16[64]{0:T(256)(128)(2,1)S(1)}, bf16[64]{0:T(256)(128)(2,1)S(1)}, u32[]{:S(2)}, u32[]{:S(2)}) collective-permute-start(bf16[64]{0:T(256)(128)(2,1)S(1)} %broadcast_select_fusion.17), channel_id=1, source_target_pairs={{0,8},{1,9},{2,10},{3,11},{4,12},{5,13},{6,14},{7,15},{8,0},{9,1},... | collective-permute-start | bytes 392 | tf_op jit(solution)/shard_map/ppermute | solution.py:209
  251.4 17.3 %collective-permute-start.13 = (bf16[24]{0:T(256)(128)(2,1)S(1)}, bf16[24]{0:T(256)(128)(2,1)S(1)}, u32[]{:S(2)}, u32[]{:S(2)}) collective-permute-start(bf16[24]{0:T(256)(128)(2,1)S(1)} %broadcast_select_fusion.13), channel_id=1, source_target_pairs={{0,1},{1,0},{2,3},{3,2},{4,5},{5,4},{6,7},{7,6},{8,9},{9,8},{10,11... | collective-permute-start | bytes 152 | tf_op jit(solution)/shard_map/ppermute | solution.py:209
  251.5 18.9 %collective-permute-start.12 = (bf16[24]{0:T(256)(128)(2,1)S(1)}, bf16[24]{0:T(256)(128)(2,1)S(1)}, u32[]{:S(2)}, u32[]{:S(2)}) collective-permute-start(bf16[24]{0:T(256)(128)(2,1)S(1)} %broadcast_select_fusion.14), channel_id=1, source_target_pairs={{0,16},{1,17},{2,18},{3,19},{4,20},{5,21},{6,22},{7,23},{8,24},{9,... | collective-permute-start | bytes 152 | tf_op jit(solution)/shard_map/ppermute | solution.py:209
  255.5 15.4 %collective-permute-start.11 = (bf16[24]{0:T(256)(128)(2,1)S(1)}, bf16[24]{0:T(256)(128)(2,1)S(1)}, u32[]{:S(2)}, u32[]{:S(2)}) collective-permute-start(bf16[24]{0:T(256)(128)(2,1)S(1)} %broadcast_select_fusion.15), channel_id=1, source_target_pairs={{0,2},{1,3},{2,0},{3,1},{4,6},{5,7},{6,4},{7,5},{8,10},{9,11},{10,... | collective-permute-start | bytes 152 | tf_op jit(solution)/shard_map/ppermute | solution.py:209
  255.6 20.7 %copy-start.4 = (s32[32,8]{1,0:T(8,128)S(1)}, s32[32,8]{1,0:T(8,128)}, u32[]{:S(2)}) copy-start(s32[32,8]{1,0:T(8,128)} %multiply_add_fusion) | copy-start | bytes 3076
  255.6 20.7 %copy-start.20 = (s32[128]{0:T(128)S(1)}, s32[128]{0:T(128)}, u32[]{:S(2)}) copy-start(s32[128]{0:T(128)} %param.25) | copy-start | bytes 1540
  255.6 17.3 %collective-permute-start.10 = (bf16[24]{0:T(256)(128)(2,1)S(1)}, bf16[24]{0:T(256)(128)(2,1)S(1)}, u32[]{:S(2)}, u32[]{:S(2)}) collective-permute-start(bf16[24]{0:T(256)(128)(2,1)S(1)} %broadcast_select_fusion.16), channel_id=1, source_target_pairs={{0,4},{1,5},{2,6},{3,7},{4,0},{5,1},{6,2},{7,3},{8,12},{9,13},{10,... | collective-permute-start | bytes 152 | tf_op jit(solution)/shard_map/ppermute | solution.py:209
  268.3 12.9 %copy-start.17 = (pred[64]{0:T(512)(128)(4,1)S(1)}, pred[64]{0:T(512)(128)(4,1)}, u32[]{:S(2)}) copy-start(pred[64]{0:T(512)(128)(4,1)} %compare_and_fusion.9) | copy-start | bytes 196
  268.8 20.1 %collective-permute-start.5 = (bf16[24,8,362]{2,1,0:T(8,128)(2,1)S(1)}, bf16[24,8,362]{2,1,0:T(8,128)(2,1)S(1)}, u32[]{:S(2)}, u32[]{:S(2)}) collective-permute-start(bf16[24,8,362]{2,1,0:T(8,128)(2,1)S(1)} %broadcast_select_fusion.11), channel_id=1, source_target_pairs={{0,4},{1,5},{2,6},{3,7},{4,0},{5,1},{6,2},{7,3},{8,12},{9,13},{10,... | collective-permute-start | bytes 417032 | tf_op jit(solution)/shard_map/ppermute | solution.py:208
  270.4 19.1 %collective-permute-start.6 = (bf16[24,8,362]{2,1,0:T(8,128)(2,1)S(1)}, bf16[24,8,362]{2,1,0:T(8,128)(2,1)S(1)}, u32[]{:S(2)}, u32[]{:S(2)}) collective-permute-start(bf16[24,8,362]{2,1,0:T(8,128)(2,1)S(1)} %broadcast_select_fusion.10), channel_id=1, source_target_pairs={{0,2},{1,3},{2,0},{3,1},{4,6},{5,7},{6,4},{7,5},{8,10},{9,11},{10,... | collective-permute-start | bytes 417032 | tf_op jit(solution)/shard_map/ppermute | solution.py:208
  270.9 19.3 %collective-permute-start.7 = (bf16[24,8,362]{2,1,0:T(8,128)(2,1)S(1)}, bf16[24,8,362]{2,1,0:T(8,128)(2,1)S(1)}, u32[]{:S(2)}, u32[]{:S(2)}) collective-permute-start(bf16[24,8,362]{2,1,0:T(8,128)(2,1)S(1)} %broadcast_select_fusion.9), channel_id=1, source_target_pairs={{0,16},{1,17},{2,18},{3,19},{4,20},{5,21},{6,22},{7,23},{8,24},{9,... | collective-permute-start | bytes 417032 | tf_op jit(solution)/shard_map/ppermute | solution.py:208
  272.9 18.0 %collective-permute-start.8 = (bf16[24,8,362]{2,1,0:T(8,128)(2,1)S(1)}, bf16[24,8,362]{2,1,0:T(8,128)(2,1)S(1)}, u32[]{:S(2)}, u32[]{:S(2)}) collective-permute-start(bf16[24,8,362]{2,1,0:T(8,128)(2,1)S(1)} %broadcast_select_fusion.8), channel_id=1, source_target_pairs={{0,1},{1,0},{2,3},{3,2},{4,5},{5,4},{6,7},{7,6},{8,9},{9,8},{10,11... | collective-permute-start | bytes 417032 | tf_op jit(solution)/shard_map/ppermute | solution.py:208
  276.3 16.0 %copy-start.16 = (f32[128]{0:T(128)}, f32[128]{0:T(128)S(1)}, u32[]{:S(2)}) copy-start(f32[128]{0:T(128)S(1)} %get-tuple-element.246) | copy-start | bytes 1540
  278.0 10.3 %all-to-all-start.1 = ((f32[32,1,8]{2,1,0:T(1,128)}), f32[32,1,8]{2,1,0:T(1,128)S(1)}, u32[]{:S(2)}, u32[]{:S(2)}) async-start(f32[32,1,8]{2,1,0:T(1,128)} %convolution_bitcast_fusion.2), calls=%async_computation.1 | async-start | bytes 32768 | tf_op jit(solution)/shard_map/all_to_all | solution.py:234
  281.4 10.2 %collective-permute-start.9 = (bf16[64,8,362]{2,1,0:T(8,128)(2,1)S(1)}, bf16[64,8,362]{2,1,0:T(8,128)(2,1)S(1)}, u32[]{:S(2)}, u32[]{:S(2)}) collective-permute-start(bf16[64,8,362]{2,1,0:T(8,128)(2,1)S(1)} %broadcast_select_fusion.7), channel_id=1, source_target_pairs={{0,8},{1,9},{2,10},{3,11},{4,12},{5,13},{6,14},{7,15},{8,0},{9,1},... | collective-permute-start | bytes 1112072 | tf_op jit(solution)/shard_map/ppermute | solution.py:208
  292.3 3.4 %copy-start = (pred[128,8,361]{0,1,2:T(8,128)(4,1)S(1)}, pred[128,8,361]{0,1,2:T(8,128)(4,1)}, u32[]{:S(2)}) copy-start(pred[128,8,361]{0,1,2:T(8,128)(4,1)} %broadcast_compare_fusion) | copy-start | bytes 1108996
  292.3 3.4 %copy-start.5 = (f32[8]{0:T(128)S(1)}, f32[8]{0:T(128)}, u32[]{:S(2)}) copy-start(f32[8]{0:T(128)} %param.33) | copy-start | bytes 100
  295.7 1.1 copy-start.6

commit v3 on v0

--- a/solution.py
+++ b/solution.py
@@ -1,13 +1,23 @@
+import functools
+
 import jax
 import jax.numpy as jnp
 from jax import lax
+from jax.experimental import pallas as pl
+from jax.experimental.pallas import tpu as pltpu
 from jax.sharding import PartitionSpec as P
 
 SIDE = 19
 BOARD = 361
+MOVES = 362
 PLANES = 32
 FACT = 8
 TREE_DEV = 8
+AXES = ("search", "net")
+CHUNK = 40
+PASSES = 3
+CORE_CAP = 64
+LINK_CAP = 28
 
 
 def convolve(inputs, kernel):
@@ -49,6 +59,50 @@
     peak = jnp.max(jnp.where(allowed, scaled, -1e30), axis=2, keepdims=True)
     weights = jnp.exp(jnp.where(allowed, scaled - peak, -1e30))
     return weights / jnp.sum(weights, axis=2, keepdims=True)
+
+
+def plan_kernel(masks, caps, counts_ref, out_ref):
+    counts_all = counts_ref[...]
+    lanes = counts_all.shape[1]
+    lane = lax.broadcasted_iota(jnp.int32, counts_all.shape, 1)
+
+    def swap(x, mask):
+        up = pltpu.roll(x, mask, 1)
+        up_from = pltpu.roll(lane, mask, 1)
+        down = pltpu.roll(x, lanes - mask, 1)
+        return jnp.where(up_from == (lane ^ mask), up, down)
+
+    flows = [jnp.zeros_like(counts_all) for _ in masks]
+    for _ in range(PASSES):
+        for e, (mask, cap) in enumerate(zip(masks, caps)):
+            sent = sum(flows)
+            got = sum(swap(f, m) for f, m in zip(flows, masks))
+            load = counts_all - sent + got
+            own = counts_all - sent
+            move = jnp.right_shift(jnp.maximum(load - swap(load, mask), 0), 1)
+            cancel = jnp.minimum(move, swap(flows[e], mask))
+            add = jnp.clip(move - cancel, 0, jnp.minimum(cap - flows[e], own))
+            flows[e] = flows[e] + add - swap(cancel, mask)
+    into = [swap(f, m) for f, m in zip(flows, masks)]
+    keep = counts_all - sum(flows)
+    starts, places = [], []
+    for e in range(len(masks)):
+        starts.append(keep + sum(flows[:e]))
+        places.append(keep + sum(into[:e]))
+    rows = flows + into + starts + places + [keep, keep + sum(into)]
+    rows = rows + [jnp.zeros_like(counts_all)] * (out_ref.shape[0] - len(rows))
+    out_ref[...] = jnp.concatenate(rows, axis=0)
+
+
+def make_plan(counts_all, masks, caps):
+    groups = counts_all.shape[0]
+    lanes = -(-groups // 128) * 128
+    padded = jnp.zeros((1, lanes), jnp.int32).at[0, :groups].set(counts_all)
+    rows = -(-(4 * len(masks) + 2) // 8) * 8
+    return pl.pallas_call(
+        functools.partial(plan_kernel, masks, caps),
+        out_shape=jax.ShapeDtypeStruct((rows, lanes), jnp.int32),
+    )(padded)
 
 
 def body(
@@ -64,39 +118,92 @@
     value_weight,
     logit_scale,
 ):
-    slot_count = states.shape[0]
+    weights = (in_weight, mid_weight, out_weight, policy_weight, pass_weight, value_weight)
+    slot_count, row = states.shape
+    groups = lax.axis_size(AXES)
+    net_size = lax.axis_size("net")
+    me = lax.axis_index(AXES)
     own_count = counts[0]
-    slot_index = jnp.arange(slot_count, dtype=jnp.int32)
-    returned_logits, returned_values = evaluate(
-        states, in_weight, mid_weight, out_weight, policy_weight, pass_weight, value_weight
-    )
-    alive = slot_index < own_count
-    priors = masked_priors(returned_logits, legal, logit_scale) * alive[:, None, None].astype(
-        jnp.float32
-    )
-    leaf_values = jnp.where(alive, returned_values.astype(jnp.float32), 0.0)
-    tree_total = TREE_DEV * lax.axis_size(("search", "net"))
+
+    counts_all = lax.all_to_all(
+        jnp.broadcast_to(counts, (groups, 1)), AXES, 0, 0, tiled=True
+    ).reshape(groups)
+
+    masks = (4, 2, 2 * net_size, 1, net_size)
+    caps = (LINK_CAP, LINK_CAP, LINK_CAP, LINK_CAP, CORE_CAP)
+    plan = make_plan(counts_all, masks, caps)
+    mine = lax.dynamic_slice(plan, (0, me), (plan.shape[0], 1))[:, 0]
+    edges = len(masks)
+    send = [mine[e] for e in range(edges)]
+    starts = [mine[2 * edges + e] for e in range(edges)]
+    places = [mine[3 * edges + e] for e in range(edges)]
+    work_count = mine[4 * edges + 1]
+
+    margin = max(caps)
+    buffer_rows = max(slot_count + margin, -(-slot_count // CHUNK) * CHUNK)
+    padded = jnp.concatenate([states, jnp.zeros((buffer_rows - slot_count, row), states.dtype)])
+    pairs = [[(d, d ^ m) for d in range(groups)] for m in masks]
+    incoming = [
+        lax.ppermute(lax.dynamic_slice(padded, (starts[e], 0), (cap, row)), AXES, pairs[e])
+        for e, cap in enumerate(caps)
+    ]
+    work = padded
+    for e in range(edges):
+        work = lax.dynamic_update_slice(work, incoming[e], (places[e], 0))
+
+    def step(t, acc):
+        rows = lax.dynamic_slice(work, (t * CHUNK, 0), (CHUNK, row))
+        logits, values = evaluate(rows, *weights)
+        column = jnp.zeros((CHUNK, 1, MOVES), jnp.bfloat16).at[:, 0, 0].set(values)
+        return lax.dynamic_update_slice(
+            acc, jnp.concatenate([logits, column], axis=1), (t * CHUNK, 0, 0)
+        )
+
+    results = lax.fori_loop(
+        0,
+        (work_count + CHUNK - 1) // CHUNK,
+        step,
+        jnp.zeros((buffer_rows, FACT + 1, MOVES), jnp.bfloat16),
+    )
+
+    final = results
+    for e, cap in enumerate(caps):
+        back = lax.ppermute(
+            lax.dynamic_slice(results, (places[e], 0, 0), (cap, FACT + 1, MOVES)), AXES, pairs[e]
+        )
+        final = lax.dynamic_update_slice(final, back, (starts[e], 0, 0))
+    slot_logits = final[:slot_count, :FACT, :]
+    slot_values = final[:slot_count, FACT, 0]
+    slot = jnp.arange(slot_count, dtype=jnp.int32)
+
+    alive = slot < own_count
+    priors = jnp.where(
+        alive[:, None, None], masked_priors(slot_logits, legal, logit_scale), 0.0
+    )
+    leaf_values = jnp.where(alive, slot_values.astype(jnp.float32), 0.0)
+    tree_total = TREE_DEV * groups
     onehot = (owners[:, None] == jnp.arange(tree_total, dtype=jnp.int32)[None, :]).astype(
         jnp.float32
     )
     partial_sums = jnp.dot(leaf_values, onehot, precision=lax.Precision.HIGHEST)
-    tree_value = lax.psum_scatter(partial_sums, ("search", "net"), scatter_dimension=0, tiled=True)
+    spread = lax.all_to_all(partial_sums.reshape(groups, TREE_DEV), AXES, 0, 0, tiled=True)
+    tree_value = jnp.sum(spread, axis=0)
     return (priors, leaf_values, tree_value)
 
 
 def solution(mesh):
     in_specs = (
-        P(("search", "net"), None),
-        P(("search", "net")),
-        P(("search", "net")),
-        P(("search", "net"), None, None),
-        P(),
-        P(),
-        P(),
-        P(),
-        P(),
-        P(),
-        P(),
-    )
-    out_specs = (P(("search", "net"), None, None), P(("search", "net")), P(("search", "net")))
+        P(AXES, None),
+        P(AXES),
+        P(AXES),
+        P(AXES, None, None),
+        P(),
+        P(),
+        P(),
+        P(),
+        P(),
+        P(),
+        P(),
+    )
+    out_specs = (P(AXES, None, None), P(AXES), P(AXES))
     return jax.shard_map(body, mesh=mesh, in_specs=in_specs, out_specs=out_specs, check_vma=False)

time: 208 us -> 543 us (2.61)
  local copies, waits for them, and re-layouts: 3.4 us -> 352 us
  matrix products: 145 us -> 56.1 us
  starting transfers between devices: 0 us -> 63.7 us
  blocking collectives: 42 us -> 0 us
  waiting for transfers between devices: 0 us -> 28.3 us
  between operations: 1.62 us -> 20.8 us
    dynamic_update_slice x0 -> x10, local copies, waits for them, and re-layouts: none -> 312 us  [the longest x5 272 us: body(): final = lax.dynamic_update_slice(final, back, (starts[e], 0, 0))]
    conv_general_dilated x3, matrix products: 139 us -> 46.3 us  [convolve(): lax.conv_general_dilated(inputs, kernel, (1, 1), 'SAME', dimension_number...]
    all_to_all x0 -> x2, starting transfers between devices: none -> 55.2 us  [the longest x1 47.9 us: body(): lax.all_to_all(partial_sums.reshape(groups, TREE_DEV), AXES, 0, 0, tiled=...]
    unnamed x1 -> x0, blocking collectives: 42 us -> none
    ppermute x0 -> x10, waiting for transfers between devices: none -> 22.1 us  [the longest x5 19.5 us: body(): lax.ppermute(lax.dynamic_slice(padded, (starts[e], 0), (cap, row)), AXES,...]
    ppermute x0 -> x5, local copies, waits for them, and re-layouts: none -> 12.3 us  [body(): lax.ppermute(lax.dynamic_slice(results, (places[e], 0, 0), (cap, FACT + 1...]
    dynamic_slice x0 -> x6, local copies, waits for them, and re-layouts: none -> 11.9 us  [the longest x2 5.49 us: step(): rows = lax.dynamic_slice(work, (t * CHUNK, 0), (CHUNK, row))]
    reduce_sum x1, other arithmetic: 12.1 us -> 0.56 us  [body(): tree_value = jnp.sum(spread, axis=0)]
  transfers between devices with their start and end apart: 0 -> 12, of which waited for: 0 -> 4; matrix products, arithmetic and copies ran while one was open for 0% -> 50% of each run, Pallas kernels for 0% -> 0%
where the time goes in v3:
time: 543 us; the launch traced here: 538 us
  local copies, waits for them, and re-layouts  352 us (65%)
  starting transfers between devices  63.7 us (12%)
  matrix products  56.1 us (10%)
  waiting for transfers between devices  28.3 us (5%)
  between operations  20.8 us (4%)
  other arithmetic  12 us (2%)
    dynamic_update_slice x5, local copies, waits for them, and re-layouts, body(): final = lax.dynamic_update_slice(final, back, (starts[e], 0, 0))  272 us
    all_to_all x1, starting transfers between devices, body(): lax.all_to_all(partial_sums.reshape(groups, TREE_DEV), AXES, 0, 0, tiled=...  47.9 us
    conv_general_dilated x3, matrix products, convolve(): lax.conv_general_dilated(inputs, kernel, (1, 1), 'SAME', dimension_number...  46.3 us
    dynamic_update_slice x5, local copies, waits for them, and re-layouts, body(): work = lax.dynamic_update_slice(work, incoming[e], (places[e], 0))  40.6 us
    ppermute x5, waiting for transfers between devices, body(): lax.ppermute(lax.dynamic_slice(padded, (starts[e], 0), (cap, row)), AXES,...  19.5 us
    ppermute x5, local copies, waits for them, and re-layouts, body(): lax.ppermute(lax.dynamic_slice(results, (places[e], 0, 0), (cap, FACT + 1...  12.3 us
  transfers between devices with their start and end apart: 12, of which 4 were waited for; matrix products, arithmetic and copies ran while one was open for 50% of the time, Pallas kernels for 0%

profile of v3, /device:TPU:0, one launch (start us, length us, event | category | flops | bytes accessed | tf_op | source)
XLA Modules:
  0.0 538.1 jit_solution(14595533264358736660)
XLA Ops:
  1.3 0.6 broadcast_in_dim.47
  1.9 7.3 %all-to-all-start = ((s32[32,1,1]{2,1,0:T(1,128)}), s32[32,1,1]{2,1,0:T(1,128)S(1)}, u32[]{:S(2)}, u32[]{:S(2)}) async-start(s32[32,1,1]{2,1,0:T(1,128)} %broadcast_in_dim.47), calls=%async_computation | async-start | bytes 32768 | tf_op jit(solution)/shard_map/all_to_all | solution.py:128
  9.2 3.4 copy.42
  12.6 0.6 compare_reduce_fusion
  13.3 3.0 all-to-all-done
  16.3 1.3 fusion.20
  17.6 0.5 scatter.6.counts_ref
  18.1 4.5 shard_map.130
  22.7 1.6 fusion.25
  31.1 1.6 pad_dynamic-slice_fusion
  35.1 2.4 pad_dynamic-slice_fusion.1
  37.5 0.6 collective-permute-start
  38.1 0.6 collective-permute-start.1
  38.8 1.5 collective-permute-start.2
  40.3 1.5 collective-permute-start.3
  41.7 2.4 concatenate.26
  54.2 19.5 %collective-permute-done = bf16[28,11552]{1,0:T(8,128)(2,1)} collective-permute-done((bf16[28,11552]{1,0:T(8,128)(2,1)}, bf16[28,11552]{1,0:T(8,128)(2,1)}, u32[]{:S(2)}, u32[]{:S(2)}) %collective-permute-start) | collective-permute-done | bytes 646944 | tf_op jit(solution)/shard_map/ppermute | solution.py:147
  73.7 7.1 %dynamic_update_slice.36 = bf16[192,11552]{1,0:T(8,128)(2,1)} dynamic-update-slice(bf16[192,11552]{1,0:T(8,128)(2,1)} %concatenate.26, bf16[28,11552]{1,0:T(8,128)(2,1)} %collective-permute-done, s32[]{:T(128)S(6)} %select_n.78, s32[]{:T(128)} %constant.138.clone.1) | dynamic-update-slice | bytes 1293828 | tf_op jit(solution)/shard_map/dynamic_update_slice | solution.py:152
  80.8 7.1 %dynamic_update_slice.37 = bf16[192,11552]{1,0:T(8,128)(2,1)} dynamic-update-slice(bf16[192,11552]{1,0:T(8,128)(2,1)} %dynamic_update_slice.36, bf16[28,11552]{1,0:T(8,128)(2,1)} %collective-permute-done.1, s32[]{:T(128)S(6)} %select_n.80, s32[]{:T(128)} %constant.138.clone.1) | dynamic-update-slice | bytes 1293828 | tf_op jit(solution)/shard_map/dynamic_update_slice | solution.py:152
  87.9 7.1 %dynamic_update_slice.38 = bf16[192,11552]{1,0:T(8,128)(2,1)} dynamic-update-slice(bf16[192,11552]{1,0:T(8,128)(2,1)} %dynamic_update_slice.37, bf16[28,11552]{1,0:T(8,128)(2,1)} %collective-permute-done.2, s32[]{:T(128)S(6)} %select_n.82, s32[]{:T(128)} %constant.138.clone.1) | dynamic-update-slice | bytes 1293828 | tf_op jit(solution)/shard_map/dynamic_update_slice | solution.py:152
  95.1 7.2 %dynamic_update_slice.39 = bf16[192,11552]{1,0:T(8,128)(2,1)} dynamic-update-slice(bf16[192,11552]{1,0:T(8,128)(2,1)} %dynamic_update_slice.38, bf16[28,11552]{1,0:T(8,128)(2,1)} %collective-permute-done.3, s32[]{:T(128)S(6)} %select_n.84, s32[]{:T(128)} %constant.138.clone.1) | dynamic-update-slice | bytes 1293828 | tf_op jit(solution)/shard_map/dynamic_update_slice | solution.py:152
  102.3 12.1 %dynamic_update_slice.40 = bf16[192,11552]{1,0:T(8,128)(2,1)} dynamic-update-slice(bf16[192,11552]{1,0:T(8,128)(2,1)} %dynamic_update_slice.39, bf16[64,11552]{1,0:T(8,128)(2,1)} %collective-permute-done.4, s32[]{:T(128)S(6)} %select_n.86, s32[]{:T(128)} %constant.138.clone.1) | dynamic-update-slice | bytes 2957316 | tf_op jit(solution)/shard_map/dynamic_update_slice | solution.py:152
  114.3 1.2 broadcast_in_dim.46
  115.6 61.2 %while.14 = (s32[]{:T(128)}, bf16[192,9,362]{2,0,1:T(8,128)(2,1)}, s32[]{:T(128)}, bf16[192,11552]{1,0:T(8,128)(2,1)}, bf16[3,3,32,256]{3,2,1,0:T(8,128)(2,1)S(1...) while((s32[]{:T(128)}, bf16[192,9,362]{2,0,1:T(8,128)(2,1)}, ...), condition=%wide.region_3.4_spmd, body=%wide.region_1.3_spmd.sunk | while | flops 33800273920 | bytes 69654072 | solution.py:162
  115.8 2.2 constant_dynamic-slice_fusion.7
  117.9 3.3 copy.58
  121.3 0.0 copy-start.5
  121.3 8.2 %maximum_convert_fusion.5 = bf16[40,19,19,256]{3,0,2,1:T(8,128)(2,1)S(1)} fusion(bf16[40,19,19,32]{0,3,2,1:T(8,128)(2,1)S(1)} %bitcast.93, bf16[3,3,32,256]{3,2,1,0:T(8,128)(2,1)S(1)} %get-tuple-element.326), kind=kOutput, calls=%fused_computation.3.clone.1 | convolution fusion | flops 1989857280 | bytes 8464896 | tf_op jit(solution)/shard_map/while/body/conv_general_dilated | solution.py:24
  129.5 18.4 %maximum_convert_fusion.6 = bf16[40,19,19,256]{3,0,2,1:T(8,128)(2,1)S(1)} fusion(bf16[40,19,19,256]{3,0,2,1:T(8,128)(2,1)S(1)} %maximum_convert_fusion.5, bf16[1,3,3,256,256]{4,3,2,1,0:T(8,128)(2,1)S(1)} %copy-done.5), kind=kOutput, calls=%fused_computation.2.clone.1 | convolution fusion | flops 15867105280 | bytes 15966208 | tf_op jit(solution)/shard_map/while/body/conv_general_dilated | solution.py:24
  147.8 19.8 %convert_reduce_fusion.2 = (f32[40,256]{1,0:T(8,128)S(1)}, bf16[40,19,19,256]{3,0,2,1:T(8,128)(2,1)}) fusion(bf16[40,19,19,256]{3,0,2,1:T(8,128)(2,1)S(1)} %maximum_convert_fusion.6, bf16[1,3,3,256,256]{4,3,2,1,0:T(8,128)(2,1)S(1)} %copy-done.6, bf16[40,19,19,256]{3,0,2,1:T(8,128)(2,1)S(1)} %maximum_convert_fusion.5), kind=kOutput, calls=%fused_computation.clone.1 | convolution fusion | flops 15881881600 | bytes 23400448 | tf_op jit(solution)/shard_map/while/body/conv_general_dilated | solution.py:24
  167.7 0.1 fusion.59
  167.8 0.2 copy.60
  168.0 0.1 fusion.58
  168.1 0.1 copy.59
  168.2 7.2 %convolution_convert_fusion.3 = bf16[40,19,19,8]{0,3,2,1:T(8,128)(2,1)S(1)} fusion(bf16[40,19,19,256]{3,0,2,1:T(8,128)(2,1)} %get-tuple-element.293, bf16[256,8]{0,1:T(8,128)(2,1)S(1)} %get-tuple-element.329), kind=kOutput, calls=%fused_computation.4.clone.1 | convolution fusion | flops 59261760 | bytes 7628416 | tf_op jit(solution)/shard_map/while/body/bhwc,cf->bfhw/dot_general | solution.py:42
  175.4 0.5 copy.61
  176.0 0.8 fusion.60
  176.8 1.2 constant_dynamic-slice_fusion.1
  178.0 0.1 collective-permute-start.9
  178.1 1.6 broadcast_compare_fusion
  179.7 1.2 constant_dynamic-slice_fusion.2
  180.9 1.3 collective-permute-start.6
  182.2 1.5 collective-permute-start.7
  183.7 1.4 collective-permute-start.8
  185.1 5.2 copy.44
  190.3 2.6 collective-permute-done.5
  192.9 3.2 copy.45
  196.1 19.0 %dynamic_update_slice.41 = bf16[192,9,362]{0,1,2:T(8,128)(2,1)} dynamic-update-slice(bf16[192,9,362]{0,1,2:T(8,128)(2,1)} %copy.44, bf16[28,9,362]{0,1,2:T(8,128)(2,1)S(1)} %copy.45, s32[]{:T(128)S(6)} %select_n.77, s32[]{:T(128)} %constant.138.clone.1, s32[]{:T(128)} %constant.138.clone.1) | dynamic-update-slice | bytes 364900 | tf_op jit(solution)/shard_map/dynamic_update_slice | solution.py:174
  215.1 3.2 copy.46
  218.3 63.2 %dynamic_update_slice.42 = bf16[192,9,362]{0,1,2:T(8,128)(2,1)} dynamic-update-slice(bf16[192,9,362]{0,1,2:T(8,128)(2,1)} %dynamic_update_slice.41, bf16[28,9,362]{0,1,2:T(8,128)(2,1)S(1)} %copy.46, s32[]{:T(128)S(6)} %select_n.79, s32[]{:T(128)} %constant.138.clone.1, s32[]{:T(128)} %constant.138.clone.1) | dynamic-update-slice | bytes 364900 | tf_op jit(solution)/shard_map/dynamic_update_slice | solution.py:174
  281.5 3.2 copy.47
  284.7 63.2 %dynamic_update_slice.43 = bf16[192,9,362]{0,1,2:T(8,128)(2,1)} dynamic-update-slice(bf16[192,9,362]{0,1,2:T(8,128)(2,1)} %dynamic_update_slice.42, bf16[28,9,362]{0,1,2:T(8,128)(2,1)S(1)} %copy.47, s32[]{:T(128)S(6)} %select_n.81, s32[]{:T(128)} %constant.138.clone.1, s32[]{:T(128)} %constant.138.clone.1) | dynamic-update-slice | bytes 364900 | tf_op jit(solution)/shard_map/dynamic_update_slice | solution.py:174
  347.9 1.4 copy.48
  349.3 63.2 %dynamic_update_slice.44 = bf16[192,9,362]{0,1,2:T(8,128)(2,1)} dynamic-update-slice(bf16[192,9,362]{0,1,2:T(8,128)(2,1)} %dynamic_update_slice.43, bf16[28,9,362]{0,1,2:T(8,128)(2,1)S(1)} %copy.48, s32[]{:T(128)S(6)} %select_n.83, s32[]{:T(128)} %constant.138.clone.1, s32[]{:T(128)} %constant.138.clone.1) | dynamic-update-slice | bytes 364900 | tf_op jit(solution)/shard_map/dynamic_update_slice | solution.py:174
  412.5 1.3 copy.49
  413.8 63.2 %dynamic_update_slice.45 = bf16[192,9,362]{0,1,2:T(8,128)(2,1)} dynamic-update-slice(bf16[192,9,362]{0,1,2:T(8,128)(2,1)} %dynamic_update_slice.44, bf16[64,9,362]{0,1,2:T(8,128)(2,1)S(1)} %copy.49, s32[]{:T(128)S(6)} %select_n.85, s32[]{:T(128)} %constant.138.clone.1, s32[]{:T(128)} %constant.138.clone.1) | dynamic-update-slice | bytes 834052 | tf_op jit(solution)/shard_map/dynamic_update_slice | solution.py:174
  477.0 1.6 select_reduce_fusion
  478.6 1.6 fusion.16
  480.2 2.3 convolution_bitcast_fusion.1
  482.5 47.9 %all-to-all-start.1 = ((f32[32,1,8]{2,1,0:T(1,128)}), f32[32,1,8]{2,1,0:T(1,128)S(1)}, u32[]{:S(2)}, u32[]{:S(2)}) async-start(f32[32,1,8]{2,1,0:T(1,128)} %convolution_bitcast_fusion.1), calls=%async_computation.1 | async-start | bytes 32768 | tf_op jit(solution)/shard_map/all_to_all | solution.py:189
  530.4 2.8 divide_select_fusion
  533.2 1.2 bitcast_select_fusion
  534.4 3.2 all-to-all-done.1
  537.5 0.6 reduce_sum.31
  (30 shorter events, 0.1 us)
Async XLA Ops:
  1.9 14.4 %all-to-all-start = ((s32[32,1,1]{2,1,0:T(1,128)}), s32[32,1,1]{2,1,0:T(1,128)S(1)}, u32[]{:S(2)}, u32[]{:S(2)}) async-start(s32[32,1,1]{2,1,0:T(1,128)} %broadcast_in_dim.47), calls=%async_computation | async-start | bytes 32768 | tf_op jit(solution)/shard_map/all_to_all | solution.py:128
  32.7 69.6 %collective-permute-start.4 = (bf16[64,11552]{1,0:T(8,128)(2,1)}, bf16[64,11552]{1,0:T(8,128)(2,1)}, u32[]{:S(2)}, u32[]{:S(2)}) collective-permute-start(bf16[64,11552]{1,0:T(8,128)(2,1)} %pad_dynamic-slice_fusion), channel_id=1, source_target_pairs={{0,8},{1,9},{2,10},{3,11},{4,12},{5,13},{6,14},{7,15},{8,0},{9,1},... | collective-permute-start | bytes 4435976 | tf_op jit(solution)/shard_map/ppermute | solution.py:147
  37.5 36.2 %collective-permute-start = (bf16[28,11552]{1,0:T(8,128)(2,1)}, bf16[28,11552]{1,0:T(8,128)(2,1)}, u32[]{:S(2)}, u32[]{:S(2)}) collective-permute-start(bf16[28,11552]{1,0:T(8,128)(2,1)} %get-tuple-element.210), channel_id=1, source_target_pairs={{0,4},{1,5},{2,6},{3,7},{4,0},{5,1},{6,2},{7,3},{8,12},{9,13},{10,... | collective-permute-start | bytes 1940744 | tf_op jit(solution)/shard_map/ppermute | solution.py:147
  38.1 42.7 %collective-permute-start.1 = (bf16[28,11552]{1,0:T(8,128)(2,1)}, bf16[28,11552]{1,0:T(8,128)(2,1)}, u32[]{:S(2)}, u32[]{:S(2)}) collective-permute-start(bf16[28,11552]{1,0:T(8,128)(2,1)} %get-tuple-element.211), channel_id=1, source_target_pairs={{0,2},{1,3},{2,0},{3,1},{4,6},{5,7},{6,4},{7,5},{8,10},{9,11},{10,... | collective-permute-start | bytes 1940744 | tf_op jit(solution)/shard_map/ppermute | solution.py:147
  38.8 49.2 %collective-permute-start.2 = (bf16[28,11552]{1,0:T(8,128)(2,1)}, bf16[28,11552]{1,0:T(8,128)(2,1)}, u32[]{:S(2)}, u32[]{:S(2)}) collective-permute-start(bf16[28,11552]{1,0:T(8,128)(2,1)} %get-tuple-element.212), channel_id=1, source_target_pairs={{0,16},{1,17},{2,18},{3,19},{4,20},{5,21},{6,22},{7,23},{8,24},{9,... | collective-permute-start | bytes 1940744 | tf_op jit(solution)/shard_map/ppermute | solution.py:147
  40.3 54.8 %collective-permute-start.3 = (bf16[28,11552]{1,0:T(8,128)(2,1)}, bf16[28,11552]{1,0:T(8,128)(2,1)}, u32[]{:S(2)}, u32[]{:S(2)}) collective-permute-start(bf16[28,11552]{1,0:T(8,128)(2,1)} %get-tuple-element.209), channel_id=1, source_target_pairs={{0,1},{1,0},{2,3},{3,2},{4,5},{5,4},{6,7},{7,6},{8,9},{9,8},{10,11... | collective-permute-start | bytes 1940744 | tf_op jit(solution)/shard_map/ppermute | solution.py:147
  95.0 20.5 %copy-start.1 = (bf16[3,3,32,256]{3,2,1,0:T(8,128)(2,1)S(1)}, bf16[3,3,32,256]{3,2,1,0:T(8,128)(2,1)}, u32[]{:S(2)}) copy-start(bf16[3,3,32,256]{3,2,1,0:T(8,128)(2,1)} %param.21) | copy-start | bytes 442372
  95.1 20.5 %copy-start.2 = (bf16[256,8]{0,1:T(8,128)(2,1)S(1)}, bf16[256,8]{0,1:T(8,128)(2,1)}, u32[]{:S(2)}) copy-start(bf16[256,8]{0,1:T(8,128)(2,1)} %param.24) | copy-start | bytes 12292
  95.1 20.5 %copy-start.3 = (bf16[256,8]{0,1:T(8,128)(2,1)S(1)}, bf16[256,8]{0,1:T(8,128)(2,1)}, u32[]{:S(2)}) copy-start(bf16[256,8]{0,1:T(8,128)(2,1)} %param.25) | copy-start | bytes 12292
  95.1 20.5 %copy-start.7 = (bf16[256]{0:T(256)(128)(2,1)S(1)}, bf16[256]{0:T(256)(128)(2,1)}, u32[]{:S(2)}) copy-start(bf16[256]{0:T(256)(128)(2,1)} %param.26) | copy-start | bytes 1540
  121.3 8.2 %copy-start.5 = (bf16[1,3,3,256,256]{4,3,2,1,0:T(8,128)(2,1)S(1)}, bf16[1,3,3,256,256]{4,3,2,1,0:T(8,128)(2,1)}, u32[]{:S(2)}) copy-start(bf16[1,3,3,256,256]{4,3,2,1,0:T(8,128)(2,1)} %get-tuple-element.327) | copy-start | bytes 3538948 | tf_op jit(solution)/shard_map/while
  129.5 18.4 %copy-start.6 = (bf16[1,3,3,256,256]{4,3,2,1,0:T(8,128)(2,1)S(1)}, bf16[1,3,3,256,256]{4,3,2,1,0:T(8,128)(2,1)}, u32[]{:S(2)}) copy-start(bf16[1,3,3,256,256]{4,3,2,1,0:T(8,128)(2,1)} %get-tuple-element.328) | copy-start | bytes 3538948 | tf_op jit(solution)/shard_map/while
  176.8 2.9 copy-start
  178.0 234.4 %collective-permute-start.9 = (bf16[64,9,362]{2,0,1:T(8,128)(2,1)S(1)}, bf16[64,9,362]{2,0,1:T(8,128)(2,1)S(1)}, u32[]{:S(2)}, u32[]{:S(2)}) collective-permute-start(bf16[64,9,362]{2,0,1:T(8,128)(2,1)S(1)} %constant_dynamic-slice_fusion.1), channel_id=1, source_target_pairs={{0,8},{1,9},{2,10},{3,11},{4,12},{5,13},{6,14},{7,15},{8,0},{9,1},... | collective-permute-start | bytes 1251080 | tf_op jit(solution)/shard_map/ppermute | solution.py:171
  180.9 11.9 %collective-permute-start.5 = (bf16[28,9,362]{2,0,1:T(8,128)(2,1)}, bf16[28,9,362]{2,0,1:T(8,128)(2,1)}, u32[]{:S(2)}, u32[]{:S(2)}) collective-permute-start(bf16[28,9,362]{2,0,1:T(8,128)(2,1)} %get-tuple-element.216), channel_id=1, source_target_pairs={{0,4},{1,5},{2,6},{3,7},{4,0},{5,1},{6,2},{7,3},{8,12},{9,13},{10,... | collective-permute-start | bytes 547352 | tf_op jit(solution)/shard_map/ppermute | solution.py:171
  180.9 34.1 %collective-permute-start.6 = (bf16[28,9,362]{2,0,1:T(8,128)(2,1)}, bf16[28,9,362]{2,0,1:T(8,128)(2,1)}, u32[]{:S(2)}, u32[]{:S(2)}) collective-permute-start(bf16[28,9,362]{2,0,1:T(8,128)(2,1)} %get-tuple-element.215), channel_id=1, source_target_pairs={{0,2},{1,3},{2,0},{3,1},{4,6},{5,7},{6,4},{7,5},{8,10},{9,11},{10,... | collective-permute-start | bytes 547352 | tf_op jit(solution)/shard_map/ppermute | solution.py:171
  182.2 99.3 %collective-permute-start.7 = (bf16[28,9,362]{2,0,1:T(8,128)(2,1)S(1)}, bf16[28,9,362]{2,0,1:T(8,128)(2,1)}, u32[]{:S(2)}, u32[]{:S(2)}) collective-permute-start(bf16[28,9,362]{2,0,1:T(8,128)(2,1)S(1)} %get-tuple-element.214), channel_id=1, source_target_pairs={{0,16},{1,17},{2,18},{3,19},{4,20},{5,21},{6,22},{7,23},{8,24},{9,... | collective-permute-start | bytes 547352 | tf_op jit(solution)/shard_map/ppermute | solution.py:171
  183.7 164.2 %collective-permute-start.8 = (bf16[28,9,362]{2,0,1:T(8,128)(2,1)S(1)}, bf16[28,9,362]{2,0,1:T(8,128)(2,1)S(1)}, u32[]{:S(2)}, u32[]{:S(2)}) collective-permute-start(bf16[28,9,362]{2,0,1:T(8,128)(2,1)S(1)} %get-tuple-element.213), channel_id=1, source_target_pairs={{0,1},{1,0},{2,3},{3,2},{4,5},{5,4},{6,7},{7,6},{8,9},{9,8},{10,11... | collective-permute-start | bytes 547352 | tf_op jit(solution)/shard_map/ppermute | solution.py:171
  412.5 64.5 %copy-start.4 = (f32[8]{0:T(128)S(1)}, f32[8]{0:T(128)}, u32[]{:S(2)}) copy-start(f32[8]{0:T(128)} %param.27) | copy-start | bytes 100
  413.8 66.4 %copy-start.8 = (s32[128]{0:T(128)S(1)}, s32[128]{0:T(128)}, u32[]{:S(2)}) copy-start(s32[128]{0:T(128)} %param.19) | copy-start | bytes 1540
  482.5 55.0 %all-to-all-start.1 = ((f32[32,1,8]{2,1,0:T(1,128)}), f32[32,1,8]{2,1,0:T(1,128)S(1)}, u32[]{:S(2)}, u32[]{:S(2)}) async-start(f32[32,1,8]{2,1,0:T(1,128)} %convolution_bitcast_fusion.1), calls=%async_computation.1 | async-start | bytes 32768 | tf_op jit(solution)/shard_map/all_to_all | solution.py:189

commit v4 on v3

--- a/solution.py
+++ b/solution.py
@@ -139,42 +139,63 @@
     places = [mine[3 * edges + e] for e in range(edges)]
     work_count = mine[4 * edges + 1]
 
+    recv = [mine[edges + e] for e in range(edges)]
+
     margin = max(caps)
-    buffer_rows = max(slot_count + margin, -(-slot_count // CHUNK) * CHUNK)
-    padded = jnp.concatenate([states, jnp.zeros((buffer_rows - slot_count, row), states.dtype)])
+    padded = jnp.concatenate([states, jnp.zeros((margin, row), states.dtype)])
     pairs = [[(d, d ^ m) for d in range(groups)] for m in masks]
     incoming = [
         lax.ppermute(lax.dynamic_slice(padded, (starts[e], 0), (cap, row)), AXES, pairs[e])
         for e, cap in enumerate(caps)
     ]
-    work = padded
-    for e in range(edges):
-        work = lax.dynamic_update_slice(work, incoming[e], (places[e], 0))
-
-    def step(t, acc):
-        rows = lax.dynamic_slice(work, (t * CHUNK, 0), (CHUNK, row))
-        logits, values = evaluate(rows, *weights)
-        column = jnp.zeros((CHUNK, 1, MOVES), jnp.bfloat16).at[:, 0, 0].set(values)
-        return lax.dynamic_update_slice(
-            acc, jnp.concatenate([logits, column], axis=1), (t * CHUNK, 0, 0)
+
+    pool = jnp.concatenate([states] + incoming, axis=0)
+    work_rows = -(-slot_count // CHUNK) * CHUNK
+    k = jnp.arange(work_rows, dtype=jnp.int32)
+    work_idx = k
+    base = slot_count
+    for e, cap in enumerate(caps):
+        inside = (k >= places[e]) & (k < places[e] + recv[e])
+        work_idx = jnp.where(inside, base + k - places[e], work_idx)
+        base = base + cap
+    work_idx = jnp.clip(work_idx, 0, pool.shape[0] - 1)
+    flat = FACT * MOVES
+
+    def step(t, carry):
+        logits_acc, values_acc = carry
+        idx = lax.dynamic_slice(work_idx, (t * CHUNK,), (CHUNK,))
+        logits, values = evaluate(jnp.take(pool, idx, axis=0), *weights)
+        logits_acc = lax.dynamic_update_slice(
+            logits_acc, logits.reshape(CHUNK, flat), (t * CHUNK, 0)
         )
-
-    results = lax.fori_loop(
+        values_acc = lax.dynamic_update_slice(values_acc, values, (t * CHUNK,))
+        return logits_acc, values_acc
+
+    work_logits, work_values = lax.fori_loop(
         0,
         (work_count + CHUNK - 1) // CHUNK,
         step,
-        jnp.zeros((buffer_rows, FACT + 1, MOVES), jnp.bfloat16),
-    )
-
-    final = results
+        (jnp.zeros((work_rows, flat), jnp.bfloat16), jnp.zeros((work_rows,), jnp.bfloat16)),
+    )
+
+    back_logits, back_values = [], []
     for e, cap in enumerate(caps):
-        back = lax.ppermute(
-            lax.dynamic_slice(results, (places[e], 0, 0), (cap, FACT + 1, MOVES)), AXES, pairs[e]
-        )
-        final = lax.dynamic_update_slice(final, back, (starts[e], 0, 0))
-    slot_logits = final[:slot_count, :FACT, :]
-    slot_values = final[:slot_count, FACT, 0]
+        idx = jnp.clip(places[e] + jnp.arange(cap, dtype=jnp.int32), 0, work_rows - 1)
+        back_logits.append(lax.ppermute(jnp.take(work_logits, idx, axis=0), AXES, pairs[e]))
+        back_values.append(lax.ppermute(jnp.take(work_values, idx, axis=0), AXES, pairs[e]))
+
+    all_logits = jnp.concatenate([work_logits] + back_logits, axis=0)
+    all_values = jnp.concatenate([work_values] + back_values, axis=0)
     slot = jnp.arange(slot_count, dtype=jnp.int32)
+    pick = slot
+    base = work_rows
+    for e, cap in enumerate(caps):
+        inside = (slot >= starts[e]) & (slot < starts[e] + send[e])
+        pick = jnp.where(inside, base + slot - starts[e], pick)
+        base = base + cap
+    pick = jnp.clip(pick, 0, all_logits.shape[0] - 1)
+    slot_logits = jnp.take(all_logits, pick, axis=0).reshape(slot_count, FACT, MOVES)
+    slot_values = jnp.take(all_values, pick, axis=0)
 
     alive = slot < own_count
     priors = jnp.where(

time: 543 us -> 248 us (0.46)
  local copies, waits for them, and re-layouts: 352 us -> 93.2 us
  starting transfers between devices: 63.7 us -> 26.8 us
  other arithmetic: 12 us -> 38.8 us
  waiting for transfers between devices: 28.3 us -> 7.29 us
  matrix products: 56.1 us -> 49.5 us
    dynamic_update_slice x10 -> x2, local copies, waits for them, and re-layouts: 312 us -> 0.24 us  [the longest x1 0.21 us: step(): values_acc = lax.dynamic_update_slice(values_acc, values, (t * CHUNK,))]
    concatenate x1 -> x3, local copies, waits for them, and re-layouts: 2.41 us -> 53 us  [the longest x1 46.1 us: body(): pool = jnp.concatenate([states] + incoming, axis=0)]
    all_to_all x1, starting transfers between devices: 47.9 us -> 2.51 us  [body(): lax.all_to_all(partial_sums.reshape(groups, TREE_DEV), AXES, 0, 0, tiled=...]
    gather x0 -> x16, local copies, waits for them, and re-layouts: none -> 25.8 us  [the longest x2 10.9 us: step(): logits, values = evaluate(jnp.take(pool, idx, axis=0), *weights)]
    ppermute x5, waiting for transfers between devices: 19.5 us -> 0.01 us  [body(): lax.ppermute(lax.dynamic_slice(padded, (starts[e], 0), (cap, row)), AXES,...]
    select_n x0 -> x15, other arithmetic: none -> 14.4 us  [the longest x8 5.18 us: body(): jnp.take(work_logits, idx, axis=0)]
    ppermute x5 -> x0, local copies, waits for them, and re-layouts: 12.3 us -> none  [body(): lax.ppermute(lax.dynamic_slice(results, (places[e], 0, 0), (cap, FACT + 1...]
    dynamic_slice x4 -> x0, local copies, waits for them, and re-layouts: 7.94 us -> none  [the longest x2 5.49 us: step(): rows = lax.dynamic_slice(work, (t * CHUNK, 0), (CHUNK, row))]
  transfers between devices with their start and end apart: 12 -> 17, of which waited for: 4 -> 2; matrix products, arithmetic and copies ran while one was open for 50% -> 15% of each run, Pallas kernels for 0% -> 0%
where the time goes in v4:
time: 248 us; the launch traced here: 245 us
  local copies, waits for them, and re-layouts  93.2 us (38%)
  matrix products  49.5 us (20%)
  other arithmetic  38.8 us (16%)
  starting transfers between devices  26.8 us (11%)
  between operations  24 us (10%)
  waiting for transfers between devices  7.29 us (3%)
  Pallas kernels  4.54 us (2%)
    concatenate x1, local copies, waits for them, and re-layouts, body(): pool = jnp.concatenate([states] + incoming, axis=0)  46.1 us
    conv_general_dilated x3, matrix products, convolve(): lax.conv_general_dilated(inputs, kernel, (1, 1), 'SAME', dimension_number...  43.5 us
    gather x2, local copies, waits for them, and re-layouts, step(): logits, values = evaluate(jnp.take(pool, idx, axis=0), *weights)  10.9 us
    all_to_all x1, starting transfers between devices, body(): lax.all_to_all(jnp.broadcast_to(counts, (groups, 1)), AXES, 0, 0, tiled=T...  7.33 us
    all_to_all x1, waiting for transfers between devices, body(): lax.all_to_all(partial_sums.reshape(groups, TREE_DEV), AXES, 0, 0, tiled=...  7.13 us
    ppermute x5, starting transfers between devices, body(): lax.ppermute(lax.dynamic_slice(padded, (starts[e], 0), (cap, row)), AXES,...  7.05 us
    concatenate x1, local copies, waits for them, and re-layouts, body(): all_logits = jnp.concatenate([work_logits] + back_logits, axis=0)  6.79 us
    ppermute x5, starting transfers between devices, body(): lax.ppermute(jnp.take(work_logits, idx, axis=0), AXES, pairs[e])  6.6 us
  transfers between devices with their start and end apart: 17, of which 2 were waited for; matrix products, arithmetic and copies ran while one was open for 15% of the time, Pallas kernels for 0%

profile of v4, /device:TPU:0, one launch (start us, length us, event | category | flops | bytes accessed | tf_op | source)
XLA Modules:
  0.0 244.6 jit_solution(5700701711702316247)
XLA Ops:
  1.9 7.3 %all-to-all-start = ((s32[32,1,1]{2,1,0:T(1,128)}), s32[32,1,1]{2,1,0:T(1,128)S(1)}, u32[]{:S(2)}, u32[]{:S(2)}) async-start(s32[32,1,1]{2,1,0:T(1,128)} %broadcast_in_dim.100), calls=%async_computation | async-start | bytes 32768 | tf_op jit(solution)/shard_map/all_to_all | solution.py:128
  9.8 2.3 broadcast_compare_fusion
  12.2 3.4 %copy.46 = bf16[128,11552]{1,0:T(8,128)(2,1)S(1)} copy(bf16[128,11552]{0,1:T(8,128)(2,1)} %param.19) | data formatting | bytes 5914624 | tf_op args[0]
  16.3 1.3 fusion.17
  18.1 4.5 %shard_map.130 = s32[24,128]{1,0:T(8,128)} custom-call(s32[1,128]{1,0:T(1,128)} %scatter.4.counts_ref), custom_call_target="tpu_custom_call" | custom-call | tf_op jit(solution)/shard_map/pallas_call | solution.py:102
  22.7 1.7 fusion.22
  27.9 1.4 fusion.23
  31.8 0.7 fusion.19
  32.5 1.2 compare_and_fusion.5
  36.1 2.4 pad_dynamic-slice_fusion.1
  38.5 2.6 %collective-permute-start = (bf16[28,11552]{1,0:T(8,128)(2,1)}, bf16[28,11552]{1,0:T(8,128)(2,1)}, u32[]{:S(2)}, u32[]{:S(2)}) collective-permute-start(bf16[28,11552]{1,0:T(8,128)(2,1)} %get-tuple-element.125), channel_id=1, source_target_pairs={{0,4},{1,5},{2,6},{3,7},{4,0},{5,1},{6,2},{7,3},{8,12},{9,13},{10,... | collective-permute-start | bytes 1940744 | tf_op jit(solution)/shard_map/ppermute | solution.py:148
  41.1 1.5 collective-permute-start.1
  42.6 1.5 collective-permute-start.2
  44.1 1.5 collective-permute-start.3
  46.2 1.6 pad_dynamic-slice_fusion
  47.8 1.2 compare_and_fusion.3
  62.1 1.3 compare_and_fusion.2
  63.4 1.2 compare_and_fusion.1
  64.5 1.2 compare_and_fusion.4
  65.8 1.3 compare_select_fusion.3
  67.1 1.3 compare_select_fusion.1
  68.4 3.3 %fusion.18 = s32[160]{0:T(256)S(1)} fusion(s32[]{:T(128)S(6)} %add.341, s32[]{:T(128)} %bitcast.29, s32[]{:T(128)S(6)} %add.338, s32[]{:T(128)} %bitcast.27, s32[]{:T(128)S(6)} %add.335, s32[]{:T(128)} %bitcast.25, s32[]{:T(128)S(6)} %add.332, s32[]{:T(128)} %bitcast.23, s32[]{:T(128)S(6)} %add.329, s32[]{:T(128)} %bitcast.21), kind=kLoop, calls=%fused_computation.100 | loop fusion | flops 4960 | bytes 680 | tf_op jit(solution)/shard_map/jit(clip)/min | solution.py:161
  72.3 3.0 %fusion.20 = s32[128]{0:T(128)S(1)} fusion(s32[]{:T(128)S(6)} %add.324, s32[]{:T(128)} %bitcast.17, s32[]{:T(128)S(6)} %add.321, s32[]{:T(128)} %bitcast.15, s32[]{:T(128)S(6)} %add.318, s32[]{:T(128)} %bitcast.13, s32[]{:T(128)S(6)} %add.315, s32[]{:T(128)} %bitcast.11, s32[]{:T(128)S(6)} %add.312, s32[]{:T(128)} %bitcast.9), kind=kLoop, calls=%fused_computation.102 | loop fusion | flops 4352 | bytes 552 | tf_op jit(solution)/shard_map/jit(_take)/jit(_where)/select_n | solution.py:197
  78.4 46.1 %concatenate.23 = bf16[304,11552]{1,0:T(8,128)(2,1)} concatenate(bf16[128,11552]{1,0:T(8,128)(2,1)S(1)} %copy.46, bf16[28,11552]{1,0:T(8,128)(2,1)} %collective-permute-done, bf16[28,11552]{1,0:T(8,128)(2,1)} %collective-permute-done.1, bf16[28,11552]{1,0:T(8,128)(2,1)} %collective-permute-done.2, bf16[28,11552]{1,0:T(8,128)(2,1)} %collective-permute-done.3, ...), dimensions={0} | concatenate | bytes 14047232 | tf_op jit(solution)/shard_map/concatenate | solution.py:152
  124.7 63.6 %while.13 = (s32[]{:T(128)}, bf16[160,2896]{1,0:T(8,128)(2,1)S(1)}, bf16[160]{0:T(256)(128)(2,1)S(1)}, s32[]{:T(128)}, s32[160]{0:T(256)S(1)}, /*index=5*/bf16[3...) while((s32[]{:T(128)}, bf16[160,2896]{1,0:T(8,128)(2,1)S(1)}, ...), condition=%wide.region_3.4_spmd, body=%wide.region_1.3_spmd.sunk | while | flops 33800157184 | bytes 72396728 | solution.py:174
  125.0 5.9 %gather_fusion = bf16[40,11552]{1,0:T(8,128)(2,1)S(1)} fusion(bf16[304,11552]{1,0:T(8,128)(2,1)} %get-tuple-element.270, s32[1024]{0:T(1024)S(1)} %pad_clamp_fusion.8), kind=kCustom, calls=%fused_computation.clone.1 | custom fusion | bytes 1848480 | tf_op jit(solution)/shard_map/while/body/jit(_take)/gather | solution.py:167
  130.9 5.0 %gather.78 = bf16[40,19,19,32]{3,2,1,0:T(8,128)(2,1)} reshape(bf16[40,11552]{1,0:T(8,128)(2,1)S(1)} %gather_fusion) | data formatting | bytes 1848320 | tf_op jit(solution)/shard_map/while/body/jit(_take)/gather | solution.py:167
  135.9 2.8 %broadcast_select_fusion.14 = bf16[40,19,19,32]{3,2,1,0:T(8,128)(2,1)S(1)} fusion(bf16[40,19,19,32]{3,2,1,0:T(8,128)(2,1)} %gather.78, pred[40]{0:T(512)(128)(4,1)S(1)} %get-tuple-element.230), kind=kLoop, calls=%fused_computation.17.clone.1 | loop fusion | flops 462080 | bytes 1848360 | tf_op jit(solution)/shard_map/while/body/jit(_take)/select_n | solution.py:167
  138.8 6.7 %maximum_convert_fusion.5 = bf16[40,19,19,256]{3,0,2,1:T(8,128)(2,1)S(1)} fusion(bf16[3,3,32,256]{3,2,1,0:T(8,128)(2,1)S(1)} %get-tuple-element.271, bf16[40,19,19,32]{3,2,1,0:T(8,128)(2,1)S(1)} %broadcast_select_fusion.14), kind=kOutput, calls=%fused_computation.16.clone.1 | convolution fusion | flops 1989857280 | bytes 8464896 | tf_op jit(solution)/shard_map/while/body/conv_general_dilated | solution.py:24
  145.5 18.3 %maximum_convert_fusion.6 = bf16[40,19,19,256]{3,0,2,1:T(8,128)(2,1)S(1)} fusion(bf16[40,19,19,256]{3,0,2,1:T(8,128)(2,1)S(1)} %maximum_convert_fusion.5, bf16[1,3,3,256,256]{4,3,2,1,0:T(8,128)(2,1)S(1)} %copy-done.14), kind=kOutput, calls=%fused_computation.15.clone.1 | convolution fusion | flops 15867105280 | bytes 15966208 | tf_op jit(solution)/shard_map/while/body/conv_general_dilated | solution.py:24
  163.8 18.6 %convert_reduce_fusion.2 = (f32[40,256]{1,0:T(8,128)S(1)}, bf16[40,19,19,256]{3,0,2,1:T(8,128)(2,1)S(1)}) fusion(bf16[40,19,19,256]{3,0,2,1:T(8,128)(2,1)S(1)} %maximum_convert_fusion.6, bf16[1,3,3,256,256]{4,3,2,1,0:T(8,128)(2,1)S(1)} %copy-done.15, bf16[40,19,19,256]{3,0,2,1:T(8,128)(2,1)S(1)} %maximum_convert_fusion.5), kind=kOutput, calls=%fused_computation.13.clone.1 | convolution fusion | flops 15881881600 | bytes 23400448 | tf_op jit(solution)/shard_map/while/body/conv_general_dilated | solution.py:24
  182.3 4.1 %convolution_convert_fusion.3 = bf16[40,19,19,8]{0,3,2,1:T(8,128)(2,1)S(1)} fusion(bf16[40,19,19,256]{3,0,2,1:T(8,128)(2,1)S(1)} %get-tuple-element.232, bf16[256,8]{0,1:T(8,128)(2,1)S(1)} %get-tuple-element.274), kind=kOutput, calls=%fused_computation.19.clone.1 | convolution fusion | flops 59261760 | bytes 7628416 | tf_op jit(solution)/shard_map/while/body/bhwc,cf->bfhw/dot_general | solution.py:42
  188.3 0.8 gather_fusion.10
  189.1 0.9 gather_fusion.3
  190.0 0.9 gather_fusion.1
  190.9 0.8 gather_fusion.6
  191.7 0.8 gather_fusion.11
  192.5 0.9 gather_fusion.7
  193.5 0.8 gather_fusion.12
  194.3 0.9 gather_fusion.8
  195.2 0.8 gather_fusion.9
  196.1 0.8 gather_fusion.5
  196.8 0.7 broadcast_select_fusion.11
  199.3 0.7 broadcast_select_fusion.9
  200.0 0.7 collective-permute-start.12
  201.3 1.4 collective-permute-start.13
  202.7 0.7 broadcast_select_fusion.12
  203.7 0.8 broadcast_select_fusion.5
  204.4 0.8 broadcast_select_fusion.4
  206.6 1.5 collective-permute-start.7
  208.1 1.4 collective-permute-start.8
  209.5 2.5 %collective-permute-start.5 = (bf16[28,2896]{1,0:T(8,128)(2,1)S(1)}, bf16[28,2896]{1,0:T(8,128)(2,1)S(1)}, u32[]{:S(2)}, u32[]{:S(2)}) collective-permute-start(bf16[28,2896]{1,0:T(8,128)(2,1)S(1)} %broadcast_select_fusion.6), channel_id=1, source_target_pairs={{0,4},{1,5},{2,6},{3,7},{4,0},{5,1},{6,2},{7,3},{8,12},{9,13},{10,... | collective-permute-start | bytes 486536 | tf_op jit(solution)/shard_map/ppermute | solution.py:184
  212.1 1.4 gather_fusion.4
  213.5 3.0 %convert_select_fusion = (f32[128]{0:T(128)S(1)}, pred[128]{0:T(512)(128)(4,1)S(1)}) fusion(bf16[128]{0:T(256)(128)(2,1)S(1)} %gather_fusion.4, s32[]{:T(128)} %bitcast.91, s32[]{:T(128)S(6)} %add.324, s32[]{:T(128)} %bitcast.17, s32[]{:T(128)S(6)} %add.321, s32[]{:T(128)} %bitcast.15, s32[]{:T(128)S(6)} %add.318, s32[]{:T(128)} %bitcast.13, s32[]{:T(128)S(6)} %add.315, ...), kind=kLoop, calls=%fused_computation.103 | loop fusion | flops 5248 | bytes 940 | tf_op jit(solution)/shard_map/jit(_where)/select_n | solution.py:204
  216.6 1.6 convolution_bitcast_fusion.1
  218.3 2.5 %all-to-all-start.1 = ((f32[32,1,8]{2,1,0:T(1,128)}), f32[32,1,8]{2,1,0:T(1,128)S(1)}, u32[]{:S(2)}, u32[]{:S(2)}) async-start(f32[32,1,8]{2,1,0:T(1,128)} %convolution_bitcast_fusion.1), calls=%async_computation.1 | async-start | bytes 32768 | tf_op jit(solution)/shard_map/all_to_all | solution.py:210
  220.8 7.1 %all-to-all-done.1 = f32[32,1,8]{2,1,0:T(1,128)S(1)} async-done(((f32[32,1,8]{2,1,0:T(1,128)}), f32[32,1,8]{2,1,0:T(1,128)S(1)}, u32[]{:S(2)}, u32[]{:S(2)}) %all-to-all-start.1) | async-done | bytes 1056 | tf_op jit(solution)/shard_map/all_to_all | solution.py:210
  228.5 0.7 copy-done.1
  229.2 0.7 copy-done.3
  229.9 6.8 %concatenate.24 = bf16[336,2896]{1,0:T(8,128)(2,1)S(1)} concatenate(bf16[160,2896]{1,0:T(8,128)(2,1)S(1)} %get-tuple-element.81, bf16[28,2896]{1,0:T(8,128)(2,1)} %copy-done.3, bf16[28,2896]{1,0:T(8,128)(2,1)S(1)} %collective-permute-done.6, bf16[28,2896]{1,0:T(8,128)(2,1)} %copy-done.1, bf16[28,2896]{1,0:T(8,128)(2,1)} %copy-done.2, bf16[64,2896]{1,0:T(8,128)(2,1)S(1)} %collective-permute-done.9), dimensions={0} | concatenate | bytes 3892224 | tf_op jit(solution)/shard_map/concatenate | solution.py:187
  236.7 2.0 gather_fusion.2
  238.7 2.3 reshape.484
  241.0 0.7 copy.48
  242.9 1.7 divide_select_fusion
  (91 shorter events, 13.7 us)
Async XLA Ops:
  1.9 14.4 %all-to-all-start = ((s32[32,1,1]{2,1,0:T(1,128)}), s32[32,1,1]{2,1,0:T(1,128)S(1)}, u32[]{:S(2)}, u32[]{:S(2)}) async-start(s32[32,1,1]{2,1,0:T(1,128)} %broadcast_in_dim.100), calls=%async_computation | async-start | bytes 32768 | tf_op jit(solution)/shard_map/all_to_all | solution.py:128
  38.5 39.9 %collective-permute-start = (bf16[28,11552]{1,0:T(8,128)(2,1)}, bf16[28,11552]{1,0:T(8,128)(2,1)}, u32[]{:S(2)}, u32[]{:S(2)}) collective-permute-start(bf16[28,11552]{1,0:T(8,128)(2,1)} %get-tuple-element.125), channel_id=1, source_target_pairs={{0,4},{1,5},{2,6},{3,7},{4,0},{5,1},{6,2},{7,3},{8,12},{9,13},{10,... | collective-permute-start | bytes 1940744 | tf_op jit(solution)/shard_map/ppermute | solution.py:148
  41.1 37.3 %collective-permute-start.1 = (bf16[28,11552]{1,0:T(8,128)(2,1)}, bf16[28,11552]{1,0:T(8,128)(2,1)}, u32[]{:S(2)}, u32[]{:S(2)}) collective-permute-start(bf16[28,11552]{1,0:T(8,128)(2,1)} %get-tuple-element.123), channel_id=1, source_target_pairs={{0,2},{1,3},{2,0},{3,1},{4,6},{5,7},{6,4},{7,5},{8,10},{9,11},{10,... | collective-permute-start | bytes 1940744 | tf_op jit(solution)/shard_map/ppermute | solution.py:148
  42.6 35.8 %collective-permute-start.2 = (bf16[28,11552]{1,0:T(8,128)(2,1)}, bf16[28,11552]{1,0:T(8,128)(2,1)}, u32[]{:S(2)}, u32[]{:S(2)}) collective-permute-start(bf16[28,11552]{1,0:T(8,128)(2,1)} %get-tuple-element.124), channel_id=1, source_target_pairs={{0,16},{1,17},{2,18},{3,19},{4,20},{5,21},{6,22},{7,23},{8,24},{9,... | collective-permute-start | bytes 1940744 | tf_op jit(solution)/shard_map/ppermute | solution.py:148
  44.1 34.4 %collective-permute-start.3 = (bf16[28,11552]{1,0:T(8,128)(2,1)}, bf16[28,11552]{1,0:T(8,128)(2,1)}, u32[]{:S(2)}, u32[]{:S(2)}) collective-permute-start(bf16[28,11552]{1,0:T(8,128)(2,1)} %get-tuple-element.122), channel_id=1, source_target_pairs={{0,1},{1,0},{2,3},{3,2},{4,5},{5,4},{6,7},{7,6},{8,9},{9,8},{10,11... | collective-permute-start | bytes 1940744 | tf_op jit(solution)/shard_map/ppermute | solution.py:148
  47.8 30.6 %collective-permute-start.4 = (bf16[64,11552]{1,0:T(8,128)(2,1)}, bf16[64,11552]{1,0:T(8,128)(2,1)}, u32[]{:S(2)}, u32[]{:S(2)}) collective-permute-start(bf16[64,11552]{1,0:T(8,128)(2,1)} %pad_dynamic-slice_fusion), channel_id=1, source_target_pairs={{0,8},{1,9},{2,10},{3,11},{4,12},{5,13},{6,14},{7,15},{8,0},{9,1},... | collective-permute-start | bytes 4435976 | tf_op jit(solution)/shard_map/ppermute | solution.py:148
  78.4 46.3 %copy-start.4 = (bf16[256,8]{0,1:T(8,128)(2,1)S(1)}, bf16[256,8]{0,1:T(8,128)(2,1)}, u32[]{:S(2)}) copy-start(bf16[256,8]{0,1:T(8,128)(2,1)} %param.26) | copy-start | bytes 12292
  78.4 46.3 %copy-start.5 = (bf16[256,8]{0,1:T(8,128)(2,1)S(1)}, bf16[256,8]{0,1:T(8,128)(2,1)}, u32[]{:S(2)}) copy-start(bf16[256,8]{0,1:T(8,128)(2,1)} %param.27) | copy-start | bytes 12292
  78.4 46.3 %copy-start.16 = (bf16[3,3,32,256]{3,2,1,0:T(8,128)(2,1)S(1)}, bf16[3,3,32,256]{3,2,1,0:T(8,128)(2,1)}, u32[]{:S(2)}) copy-start(bf16[3,3,32,256]{3,2,1,0:T(8,128)(2,1)} %param.23) | copy-start | bytes 442372
  78.4 46.3 %copy-start.17 = (bf16[256]{0:T(256)(128)(2,1)S(1)}, bf16[256]{0:T(256)(128)(2,1)}, u32[]{:S(2)}) copy-start(bf16[256]{0:T(256)(128)(2,1)} %param.28) | copy-start | bytes 1540
  138.8 6.7 %copy-start.14 = (bf16[1,3,3,256,256]{4,3,2,1,0:T(8,128)(2,1)S(1)}, bf16[1,3,3,256,256]{4,3,2,1,0:T(8,128)(2,1)}, u32[]{:S(2)}) copy-start(bf16[1,3,3,256,256]{4,3,2,1,0:T(8,128)(2,1)} %get-tuple-element.272) | copy-start | bytes 3538948 | tf_op jit(solution)/shard_map/while
  145.5 18.3 %copy-start.15 = (bf16[1,3,3,256,256]{4,3,2,1,0:T(8,128)(2,1)S(1)}, bf16[1,3,3,256,256]{4,3,2,1,0:T(8,128)(2,1)}, u32[]{:S(2)}) copy-start(bf16[1,3,3,256,256]{4,3,2,1,0:T(8,128)(2,1)} %get-tuple-element.273) | copy-start | bytes 3538948 | tf_op jit(solution)/shard_map/while
  192.5 11.0 %copy-start.8 = (pred[64]{0:T(512)(128)(4,1)S(1)}, pred[64]{0:T(512)(128)(4,1)}, u32[]{:S(2)}) copy-start(pred[64]{0:T(512)(128)(4,1)} %compare_and_fusion.5) | copy-start | bytes 196
  193.4 10.2 %copy-start.9 = (pred[28]{0:T(512)(128)(4,1)S(1)}, pred[28]{0:T(512)(128)(4,1)}, u32[]{:S(2)}) copy-start(pred[28]{0:T(512)(128)(4,1)} %compare_and_fusion.3) | copy-start | bytes 88
  193.4 11.0 %copy-start.12 = (pred[28]{0:T(512)(128)(4,1)S(1)}, pred[28]{0:T(512)(128)(4,1)}, u32[]{:S(2)}) copy-start(pred[28]{0:T(512)(128)(4,1)} %compare_and_fusion.2) | copy-start | bytes 88
  193.4 11.8 %copy-start.11 = (pred[28]{0:T(512)(128)(4,1)S(1)}, pred[28]{0:T(512)(128)(4,1)}, u32[]{:S(2)}) copy-start(pred[28]{0:T(512)(128)(4,1)} %compare_and_fusion.1) | copy-start | bytes 88
  194.3 11.0 %copy-start.10 = (pred[28]{0:T(512)(128)(4,1)S(1)}, pred[28]{0:T(512)(128)(4,1)}, u32[]{:S(2)}) copy-start(pred[28]{0:T(512)(128)(4,1)} %compare_and_fusion.4) | copy-start | bytes 88
  194.3 22.3 %copy-start.6 = (s32[32,8]{1,0:T(8,128)S(1)}, s32[32,8]{1,0:T(8,128)}, u32[]{:S(2)}) copy-start(s32[32,8]{1,0:T(8,128)} %multiply_add_fusion) | copy-start | bytes 3076
  194.3 22.3 %copy-start.18 = (s32[128]{0:T(128)S(1)}, s32[128]{0:T(128)}, u32[]{:S(2)}) copy-start(s32[128]{0:T(128)} %param.21) | copy-start | bytes 1540
  197.5 7.9 %collective-permute-start.10 = (bf16[28]{0:T(256)(128)(2,1)S(1)}, bf16[28]{0:T(256)(128)(2,1)S(1)}, u32[]{:S(2)}, u32[]{:S(2)}) collective-permute-start(bf16[28]{0:T(256)(128)(2,1)S(1)} %broadcast_select_fusion.11), channel_id=1, source_target_pairs={{0,4},{1,5},{2,6},{3,7},{4,0},{5,1},{6,2},{7,3},{8,12},{9,13},{10,... | collective-permute-start | bytes 176 | tf_op jit(solution)/shard_map/ppermute | solution.py:185
  198.7 7.3 %collective-permute-start.11 = (bf16[28]{0:T(256)(128)(2,1)S(1)}, bf16[28]{0:T(256)(128)(2,1)S(1)}, u32[]{:S(2)}, u32[]{:S(2)}) collective-permute-start(bf16[28]{0:T(256)(128)(2,1)S(1)} %broadcast_select_fusion.10), channel_id=1, source_target_pairs={{0,2},{1,3},{2,0},{3,1},{4,6},{5,7},{6,4},{7,5},{8,10},{9,11},{10,... | collective-permute-start | bytes 176 | tf_op jit(solution)/shard_map/ppermute | solution.py:185
  200.0 6.6 %collective-permute-start.12 = (bf16[28]{0:T(256)(128)(2,1)S(1)}, bf16[28]{0:T(256)(128)(2,1)S(1)}, u32[]{:S(2)}, u32[]{:S(2)}) collective-permute-start(bf16[28]{0:T(256)(128)(2,1)S(1)} %broadcast_select_fusion.9), channel_id=1, source_target_pairs={{0,16},{1,17},{2,18},{3,19},{4,20},{5,21},{6,22},{7,23},{8,24},{9,... | collective-permute-start | bytes 176 | tf_op jit(solution)/shard_map/ppermute | solution.py:185
  201.3 6.8 %collective-permute-start.13 = (bf16[28]{0:T(256)(128)(2,1)S(1)}, bf16[28]{0:T(256)(128)(2,1)S(1)}, u32[]{:S(2)}, u32[]{:S(2)}) collective-permute-start(bf16[28]{0:T(256)(128)(2,1)S(1)} %broadcast_select_fusion.8), channel_id=1, source_target_pairs={{0,1},{1,0},{2,3},{3,2},{4,5},{5,4},{6,7},{7,6},{8,9},{9,8},{10,11... | collective-permute-start | bytes 176 | tf_op jit(solution)/shard_map/ppermute | solution.py:185
  203.4 6.1 %collective-permute-start.14 = (bf16[64]{0:T(256)(128)(2,1)S(1)}, bf16[64]{0:T(256)(128)(2,1)S(1)}, u32[]{:S(2)}, u32[]{:S(2)}) collective-permute-start(bf16[64]{0:T(256)(128)(2,1)S(1)} %broadcast_select_fusion.12), channel_id=1, source_target_pairs={{0,8},{1,9},{2,10},{3,11},{4,12},{5,13},{6,14},{7,15},{8,0},{9,1},... | collective-permute-start | bytes 392 | tf_op jit(solution)/shard_map/ppermute | solution.py:185
  205.4 24.5 %collective-permute-start.9 = (bf16[64,2896]{1,0:T(8,128)(2,1)S(1)}, bf16[64,2896]{1,0:T(8,128)(2,1)S(1)}, u32[]{:S(2)}, u32[]{:S(2)}) collective-permute-start(bf16[64,2896]{1,0:T(8,128)(2,1)S(1)} %broadcast_select_fusion.2), channel_id=1, source_target_pairs={{0,8},{1,9},{2,10},{3,11},{4,12},{5,13},{6,14},{7,15},{8,0},{9,1},... | collective-permute-start | bytes 1112072 | tf_op jit(solution)/shard_map/ppermute | solution.py:184
  206.0 22.5 %collective-permute-start.6 = (bf16[28,2896]{1,0:T(8,128)(2,1)}, bf16[28,2896]{1,0:T(8,128)(2,1)S(1)}, u32[]{:S(2)}, u32[]{:S(2)}) collective-permute-start(bf16[28,2896]{1,0:T(8,128)(2,1)} %broadcast_select_fusion.5), channel_id=1, source_target_pairs={{0,2},{1,3},{2,0},{3,1},{4,6},{5,7},{6,4},{7,5},{8,10},{9,11},{10,... | collective-permute-start | bytes 486536 | tf_op jit(solution)/shard_map/ppermute | solution.py:184
  206.6 21.9 %collective-permute-start.7 = (bf16[28,2896]{1,0:T(8,128)(2,1)}, bf16[28,2896]{1,0:T(8,128)(2,1)S(1)}, u32[]{:S(2)}, u32[]{:S(2)}) collective-permute-start(bf16[28,2896]{1,0:T(8,128)(2,1)} %broadcast_select_fusion.4), channel_id=1, source_target_pairs={{0,16},{1,17},{2,18},{3,19},{4,20},{5,21},{6,22},{7,23},{8,24},{9,... | collective-permute-start | bytes 486536 | tf_op jit(solution)/shard_map/ppermute | solution.py:184
  208.1 20.4 %collective-permute-start.8 = (bf16[28,2896]{1,0:T(8,128)(2,1)S(1)}, bf16[28,2896]{1,0:T(8,128)(2,1)S(1)}, u32[]{:S(2)}, u32[]{:S(2)}) collective-permute-start(bf16[28,2896]{1,0:T(8,128)(2,1)S(1)} %broadcast_select_fusion.3), channel_id=1, source_target_pairs={{0,1},{1,0},{2,3},{3,2},{4,5},{5,4},{6,7},{7,6},{8,9},{9,8},{10,11... | collective-permute-start | bytes 486536 | tf_op jit(solution)/shard_map/ppermute | solution.py:184
  209.5 19.0 %collective-permute-start.5 = (bf16[28,2896]{1,0:T(8,128)(2,1)S(1)}, bf16[28,2896]{1,0:T(8,128)(2,1)S(1)}, u32[]{:S(2)}, u32[]{:S(2)}) collective-permute-start(bf16[28,2896]{1,0:T(8,128)(2,1)S(1)} %broadcast_select_fusion.6), channel_id=1, source_target_pairs={{0,4},{1,5},{2,6},{3,7},{4,0},{5,1},{6,2},{7,3},{8,12},{9,13},{10,... | collective-permute-start | bytes 486536 | tf_op jit(solution)/shard_map/ppermute | solution.py:184
  216.6 22.1 %copy-start.13 = (f32[128]{0:T(128)}, f32[128]{0:T(128)S(1)}, u32[]{:S(2)}) copy-start(f32[128]{0:T(128)S(1)} %get-tuple-element.118) | copy-start | bytes 1540
  218.3 9.7 %all-to-all-start.1 = ((f32[32,1,8]{2,1,0:T(1,128)}), f32[32,1,8]{2,1,0:T(1,128)S(1)}, u32[]{:S(2)}, u32[]{:S(2)}) async-start(f32[32,1,8]{2,1,0:T(1,128)} %convolution_bitcast_fusion.1), calls=%async_computation.1 | async-start | bytes 32768 | tf_op jit(solution)/shard_map/all_to_all | solution.py:210
  228.5 0.7 copy-start.1
  228.5 0.7 copy-start.2
  229.2 0.7 copy-start.3
  238.7 3.0 %copy-start = (pred[128,8,361]{0,1,2:T(8,128)(4,1)S(1)}, pred[128,8,361]{0,1,2:T(8,128)(4,1)}, u32[]{:S(2)}) copy-start(pred[128,8,361]{0,1,2:T(8,128)(4,1)} %broadcast_compare_fusion) | copy-start | bytes 1108996
  238.7 3.0 %copy-start.7 = (f32[8]{0:T(128)S(1)}, f32[8]{0:T(128)}, u32[]{:S(2)}) copy-start(f32[8]{0:T(128)} %param.29) | copy-start | bytes 100
